TPU v7x, 512 devices: a whole 4x4x16 slice. The times are simulated.
512 devices in a mesh: group: 32 (over z, core), vocab: 16 (over y, x).
Axes of the slice: x: 4, y: 4, z: 16, core: 2. Of those that a mesh axis runs over, the one named last changes fastest.
Arguments:
- hidden_in: bfloat16 [2, 2048, 2048], P(None, 'group'), may hold values from -6 to 6
- qkv_weight: bfloat16 [2, 2048, 6144], P(None, 'group', 'vocab'), may hold values from -0.125 to 0.125
- out_weight: bfloat16 [2, 2048, 2048], P(None, 'vocab', 'group'), may hold values from -0.125 to 0.125
- q_gain: float32 [2, 2048], P(None, 'vocab'), may hold values from 0.1 to 1.9
- k_gain: float32 [2, 2048], P(None, 'vocab'), may hold values from 0.1 to 1.9
- post_gain: float32 [2, 2048], replicated, may hold values from 0.1 to 1.9
- final_gain: float32 [2, 2048], replicated, may hold values from 0.1 to 1.9
- head_weight: bfloat16 [2, 2048, 100352], P(None, None, ('group', 'vocab'))
- pool_keys: bfloat16 [2, 2048, 16, 2048], P(None, 'group', None, 'vocab'), may hold values from -160 to 160
- pool_values: bfloat16 [2, 2048, 16, 2048], P(None, 'group', None, 'vocab'), may hold values from -6 to 6
- page_table: int32 [64, 32], replicated, may hold values from 0 to 2047, as said below
- deal: int32 [64], replicated, may hold values from 0 to 63, each once
- prompt_len: int32 [64], replicated, may hold values from 1 to 512, 13107 in all
- segment_ids: int32 [32, 64], replicated, may hold values from 0 to 1, never falling along the last dimension, each value on 1 to 48 neighbouring positions
- targets: int32 [2048], replicated, may hold values from 0 to 100351
- owners: int32 [64], replicated, may hold values from 0 to 63, each once
Outputs:
- hidden_out: bfloat16 [2, 2048, 2048], P(None, 'group', 'vocab')
- token_logprobs: float32 [2, 2048], P(None, 'group')
- seq_diff: float32 [64], P('group')
Inputs may be any that keep to these rules, and one draw needn't show every extreme that they name: `page_table`: entry j of a request's row is a page held by group j mod (32); every page of the pool appears exactly once. `deal`: each request appears once. `owners`: each slot appears once. `segment_ids`: each row numbers its 2 sequences in order, every one present.
All inputs are finite; a program needn't handle non-finite values.
Results may differ from a plain program's by a relative error of at most 0.017.
The roundings to bfloat16 on the way count: a program that leaves them out, or rounds other values in their place, can miss the bound.
Values may be sent and summed in bfloat16 or wider, within the bound.
No kernel may reach another device: no remote copies, remote signals or barrier semaphores. Data moves between devices by JAX's collectives and lax.ppermute only.
A program may use at most 192 MiB of HBM per device.

v0:
```python
import math

import jax
import jax.numpy as jnp
from jax import lax
from jax.sharding import PartitionSpec as P

D = 2048
HEADS = 16
TOK_G = 64
SEQ_G = 2
PPG = 1


EPS = 1e-06
THETA = 500000.0
MASKED = -1e30


def rms_scale(values, gain):
    mean_sq = jnp.mean(values * values, axis=-1, keepdims=True)
    return values * lax.rsqrt(mean_sq + EPS) * gain


def rotate(values, positions):
    half = values.shape[-1] // 2
    freq = THETA ** (-(jnp.arange(half, dtype=jnp.float32) * 2.0 / values.shape[-1]))
    angle = positions[:, None] * freq[None, :]
    cosine = jnp.concatenate([jnp.cos(angle), jnp.cos(angle)], axis=-1)[:, None, :]
    sine = jnp.concatenate([jnp.sin(angle), jnp.sin(angle)], axis=-1)[:, None, :]
    rolled = jnp.concatenate([-values[..., half:], values[..., :half]], axis=-1)
    return values * cosine + rolled * sine


def pick_small(table, index):
    match = jnp.arange(table.shape[0], dtype=jnp.int32)[None, :] == index[:, None]
    return jnp.sum(jnp.where(match, table[None, :], 0), axis=1)


def blend(first, second):
    top_one, mass_one, sum_one = first
    top_two, mass_two, sum_two = second
    highest = jnp.maximum(top_one, top_two)
    weight_one = jnp.exp(top_one - highest)
    weight_two = jnp.exp(top_two - highest)
    return (
        highest,
        mass_one * weight_one + mass_two * weight_two,
        sum_one * weight_one[..., None] + sum_two * weight_two[..., None],
    )


def shards(
    hidden_in,
    qkv_weight,
    out_weight,
    q_gain,
    k_gain,
    post_gain,
    final_gain,
    head_weight,
    pool_keys,
    pool_values,
    page_table,
    deal,
    prompt_len,
    segment_ids,
    targets,
    owners,
):
    groups = lax.axis_size("group")
    vocab_count = lax.axis_size("vocab")
    group_idx = lax.axis_index("group")
    vocab_idx = lax.axis_index("vocab")
    head_size = D // HEADS
    heads_dev = HEADS // vocab_count
    score_scale = 1.0 / math.sqrt(head_size)
    request_count = deal.shape[0]
    united = jnp.einsum(
        "mtd,mdc->mtc",
        hidden_in,
        lax.all_gather(qkv_weight, "group", axis=1, tiled=True),
        preferred_element_type=jnp.float32,
    )
    united = united.reshape(2, TOK_G, heads_dev, 3, head_size)
    query_raw = united[:, :, :, 0, :].reshape(2, TOK_G, heads_dev * head_size)
    key_raw = united[:, :, :, 1, :].reshape(2, TOK_G, heads_dev * head_size)
    query_sq, key_sq = lax.psum(
        (jnp.sum(query_raw * query_raw, axis=-1), jnp.sum(key_raw * key_raw, axis=-1)), "vocab"
    )
    query_normed = query_raw * lax.rsqrt(query_sq[..., None] / D + EPS) * q_gain[:, None, :]
    key_normed = key_raw * lax.rsqrt(key_sq[..., None] / D + EPS) * k_gain[:, None, :]
    seg_ids = lax.dynamic_index_in_dim(segment_ids, group_idx, 0, keepdims=False)
    requests = lax.dynamic_slice_in_dim(deal, group_idx * SEQ_G, SEQ_G)
    seq_numbers = jnp.arange(SEQ_G, dtype=jnp.int32)
    token_index = jnp.arange(TOK_G, dtype=jnp.int32)
    onehot = seg_ids[:, None] == seq_numbers[None, :]
    starts = jnp.sum((seg_ids[None, :] < seq_numbers[:, None]).astype(jnp.int32), axis=1)
    prompt_rows = pick_small(prompt_len, requests)
    tok_start = jnp.sum(jnp.where(onehot, starts[None, :], 0), axis=1)
    tok_prompt = jnp.sum(jnp.where(onehot, prompt_rows[None, :], 0), axis=1)
    positions = (tok_prompt + token_index - tok_start).astype(jnp.float32)
    queries = rotate(query_normed.reshape(2, TOK_G, heads_dev, head_size), positions).astype(
        jnp.bfloat16
    )
    new_keys = rotate(key_normed.reshape(2, TOK_G, heads_dev, head_size), positions).astype(
        jnp.bfloat16
    )
    new_values = united[:, :, :, 2, :].astype(jnp.bfloat16)
    pages_here = pool_keys.shape[1]
    dealt = jnp.take(page_table, deal, axis=0).reshape(groups, SEQ_G, PPG, groups)
    local_pages = (
        lax.dynamic_index_in_dim(dealt, group_idx, 3, keepdims=False) - group_idx * pages_here
    )
    order = jnp.transpose(local_pages, (1, 2, 0))
    send_keys = jnp.take(pool_keys, order, axis=1)
    send_values = jnp.take(pool_values, order, axis=1)
    got_keys, got_values = (
        lax.all_to_all(send_keys, "group", split_axis=3, concat_axis=3, tiled=True),
        lax.all_to_all(send_values, "group", split_axis=3, concat_axis=3, tiled=True),
    )
    cache_rows = got_keys.shape[2] * got_keys.shape[3] * got_keys.shape[4]
    cache_keys = got_keys.reshape(2, SEQ_G, cache_rows, heads_dev, head_size)
    cache_values = got_values.reshape(2, SEQ_G, cache_rows, heads_dev, head_size).astype(
        jnp.float32
    )
    valid = jnp.arange(cache_rows, dtype=jnp.int32)[None, :] < prompt_rows[:, None]
    cache_mask = (onehot[:, :, None] & valid[None, :, :])[None, :, None, :, :]
    cache_scores = (
        jnp.einsum("mthd,mslhd->mthsl", queries, cache_keys, preferred_element_type=jnp.float32)
        * score_scale
    )
    cache_scores = jnp.where(cache_mask, cache_scores, MASKED)
    peak_cache = jnp.max(cache_scores, axis=(3, 4))
    cache_weights = jnp.where(cache_mask, jnp.exp(cache_scores - peak_cache[..., None, None]), 0.0)
    mass_cache = jnp.sum(cache_weights, axis=(3, 4))
    sum_cache = jnp.einsum("mthsl,mslhd->mthd", cache_weights, cache_values)
    same_seq = (seg_ids[:, None] == seg_ids[None, :]) & (
        token_index[None, :] <= token_index[:, None]
    )
    self_mask = same_seq[None, :, None, :]
    self_scores = (
        jnp.einsum("mthd,muhd->mthu", queries, new_keys, preferred_element_type=jnp.float32)
        * score_scale
    )
    self_scores = jnp.where(self_mask, self_scores, MASKED)
    peak_self = jnp.max(self_scores, axis=3)
    self_weights = jnp.where(self_mask, jnp.exp(self_scores - peak_self[..., None]), 0.0)
    mass_self = jnp.sum(self_weights, axis=3)
    sum_self = jnp.einsum("mthu,muhd->mthd", self_weights, new_values.astype(jnp.float32))
    peak_both, mass_both, sum_both = blend(
        (peak_cache, mass_cache, sum_cache), (peak_self, mass_self, sum_self)
    )
    attended = (
        (sum_both / mass_both[..., None])
        .reshape(2, TOK_G, heads_dev * head_size)
        .astype(jnp.bfloat16)
    )
    partial_mix = jnp.einsum(
        "mtc,mcd->mtd",
        attended,
        lax.all_gather(out_weight, "group", axis=2, tiled=True),
        preferred_element_type=jnp.float32,
    )
    mixed = lax.psum(partial_mix, "vocab")
    hidden_new = (hidden_in.astype(jnp.float32) + rms_scale(mixed, post_gain[:, None, :])).astype(
        jnp.bfloat16
    )
    col_width = D // vocab_count
    hidden_out = lax.dynamic_slice_in_dim(hidden_new, vocab_idx * col_width, col_width, 2)
    final = rms_scale(hidden_new.astype(jnp.float32), final_gain[:, None, :]).astype(jnp.bfloat16)
    voc_here = head_weight.shape[2]
    first_column = (group_idx * vocab_count + vocab_idx) * voc_here
    logits = jnp.einsum(
        "mtd,mdv->mtv",
        lax.all_gather(final, "group", axis=1, tiled=True),
        head_weight,
        preferred_element_type=jnp.float32,
    )
    highest = jnp.max(logits, axis=-1)
    exp_sum = jnp.sum(jnp.exp(logits - highest[..., None]), axis=-1)
    wanted = targets - first_column
    found = jnp.arange(voc_here, dtype=jnp.int32)[None, :] == wanted[:, None]
    picked = jnp.sum(jnp.where(found[None], logits, 0.0), axis=-1)
    statistics = jnp.stack((highest, exp_sum, picked), axis=1)
    local_peak = statistics[:, 0]
    local_mass = statistics[:, 1]
    local_target = statistics[:, 2]
    peak_logit = lax.pmax(local_peak, ("group", "vocab"))
    exp_total, target_logit = lax.psum(
        (local_mass * jnp.exp(local_peak - peak_logit), local_target), ("group", "vocab")
    )
    logprobs = target_logit - (peak_logit + jnp.log(exp_total))
    own_logprobs = lax.dynamic_slice_in_dim(logprobs, group_idx * TOK_G, TOK_G, 1)
    gap = own_logprobs[0] - own_logprobs[1]
    onehot_wide = onehot.astype(jnp.float32)
    means = jnp.sum(onehot_wide * gap[:, None], axis=0) / jnp.sum(onehot_wide, axis=0)
    slots = pick_small(owners, requests)
    spread = jnp.sum(
        jnp.where(
            jnp.arange(request_count, dtype=jnp.int32)[None, :] == slots[:, None],
            means[:, None],
            0.0,
        ),
        axis=0,
    )
    seq_diff = lax.psum_scatter(spread, "group", scatter_dimension=0, tiled=True)
    return (hidden_out, own_logprobs, seq_diff)


def solution(mesh):
    return jax.shard_map(
        shards,
        mesh=mesh,
        in_specs=(
            P(None, "group", None),
            P(None, "group", "vocab"),
            P(None, "vocab", "group"),
            P(None, "vocab"),
            P(None, "vocab"),
            P(),
            P(),
            P(None, None, ("group", "vocab")),
            P(None, "group", None, "vocab"),
            P(None, "group", None, "vocab"),
            P(),
            P(),
            P(),
            P(),
            P(),
            P(),
        ),
        out_specs=(P(None, "group", "vocab"), P(None, "group"), P("group")),
        check_vma=False,
    )
```

profile of v0, /device:TPU:1, one launch (start us, length us, event | category | flops | bytes accessed | tf_op | source)
XLA Modules:
  0.0 678.4 jit_solution(14024238218905324672)
XLA Ops:
  7.9 0.8 copy.61
  11.2 1.7 gather_fusion.2
  12.9 1.7 gather_fusion.1
  14.9 0.9 copy.63
  15.7 16.7 %all-to-all-start = ((bf16[2,2,1,32,16,128]{5,4,1,0,2,3:T(8,128)(2,1)}), bf16[2,2,1,32,16,128]{5,4,1,0,2,3:T(8,128)(2,1)S(1)}, u32[]{:S(2)}, u32[]{:S(2)}) async-start(bf16[2,2,1,32,16,128]{5,4,1,0,2,3:T(8,128)(2,1)} %copy.63), calls=%async_computation | async-start | bytes 1048576 | tf_op jit(solution)/shard_map/all_to_all | solution.py:120
  32.5 0.9 copy.65
  33.3 38.1 %all-to-all-done = bf16[2,2,1,32,16,128]{5,4,1,0,2,3:T(8,128)(2,1)S(1)} async-done(((bf16[2,2,1,32,16,128]{5,4,1,0,2,3:T(8,128)(2,1)}), bf16[2,2,1,32,16,128]{5,4,1,0,2,3:T(8,128)(2,1)S(1)}, u32[]{:S(2)}, u32[]{:S(2)}) %all-to-all-start) | async-done | bytes 524320 | tf_op jit(solution)/shard_map/all_to_all | solution.py:120
  71.4 4.3 all-to-all-start.1
  78.4 33.4 %all-to-all-done.1 = bf16[2,2,1,32,16,128]{5,4,1,0,2,3:T(8,128)(2,1)S(1)} async-done(((bf16[2,2,1,32,16,128]{5,4,1,0,2,3:T(8,128)(2,1)}), bf16[2,2,1,32,16,128]{5,4,1,0,2,3:T(8,128)(2,1)S(1)}, u32[]{:S(2)}, u32[]{:S(2)}) %all-to-all-start.1) | async-done | bytes 524320 | tf_op jit(solution)/shard_map/all_to_all | solution.py:119
  111.8 2.6 fusion.70
  114.9 33.6 %all-reduce.2 = (f32[2,64]{1,0:T(2,128)S(1)}, f32[2,64]{1,0:T(2,128)S(1)}) all-reduce(f32[2,64]{1,0:T(2,128)S(1)} %get-tuple-element.40, f32[2,64]{1,0:T(2,128)S(1)} %get-tuple-element.41), channel_id=1, replica_groups=mesh['group'=32,'vocab'=16] {'vocab'}, use_global_device_ids=true, to_apply=%region_2.4 | all-reduce | flops 256 | bytes 2048 | tf_op jit(solution)/shard_map/psum | solution.py:88
  150.2 29.3 %all-gather.6.cloned.1.call-done = bf16[2,128,2048]{1,2,0:T(8,128)(2,1)} async-done(((bf16[2,128,64]{1,2,0:T(8,128)(2,1)}), bf16[2,128,2048]{1,2,0:T(8,128)(2,1)}) %all-gather.6.cloned.1.call-update) | async-done | bytes 1048592 | tf_op jit(solution)/shard_map/all_gather | solution.py:162
  179.5 2.9 fusion.15
  182.4 113.8 %all-reduce.5.cloned.1.call-done = f32[2,64,2048]{2,1,0:T(8,128)} async-done(((f32[2,64,2048]{2,1,0:T(8,128)}), f32[2,64,2048]{2,1,0:T(8,128)}) %all-reduce.5.cloned.1.call-update) | async-done | bytes 1048592 | tf_op jit(solution)/shard_map/psum | solution.py:165
  296.2 1.4 multiply_reduce_fusion
  297.6 1.6 fusion.12
  299.2 1.0 fusion.14
  300.2 1.3 dynamic-slice
  303.1 105.3 %all-gather.8.cloned.1.call-done = bf16[2,2048,2048]{2,1,0:T(8,128)(2,1)} async-done(((bf16[2,64,2048]{2,1,0:T(8,128)(2,1)}), bf16[2,2048,2048]{2,1,0:T(8,128)(2,1)}) %all-gather.8.cloned.1.call-update) | async-done | bytes 16777232 | tf_op jit(solution)/shard_map/all_gather | solution.py:176
  408.4 11.1 %fusion.69 = (f32[2,2048]{1,0:T(2,128)S(1)}, f32[2,2048,196]{1,2,0:T(8,128)}) fusion(bf16[2,2048,2048]{2,1,0:T(8,128)(2,1)} %all-gather.8.cloned.1.call-done, bf16[2,2048,196]{1,0,2:T(2,128)(2,1)S(1)} %copy-done), kind=kOutput, calls=%fused_computation.130 | convolution fusion | flops 3289133056 | bytes 21610496 | tf_op jit(solution)/shard_map/mtd,mdv->mtv/dot_general | solution.py:174
  419.5 103.3 %pmax.7 = f32[2,2048]{1,0:T(2,128)S(1)} all-reduce(f32[2,2048]{1,0:T(2,128)S(1)} %get-tuple-element.37), channel_id=1, replica_groups=mesh['group'=32,'vocab'=16] {'group','vocab'}, use_global_device_ids=true, to_apply=%region_18.20 | all-reduce | flops 4096 | bytes 32768 | tf_op jit(solution)/shard_map/pmax | solution.py:189
  522.8 2.8 exponential_reduce_fusion
  525.6 99.5 %all-reduce.1 = (f32[2,2048]{1,0:T(2,128)S(1)}, f32[2,2048]{1,0:T(2,128)S(1)}) all-reduce(f32[2,2048]{1,0:T(2,128)S(1)} %get-tuple-element.5, f32[2,2048]{1,0:T(2,128)S(1)} %exponential_multiply_fusion), channel_id=1, replica_groups=mesh['group'=32,'vocab'=16] {'group','vocab'}, use_global_device_ids=true, to_apply=%region_16.18 | all-reduce | flops 8192 | bytes 65536 | tf_op jit(solution)/shard_map/psum | solution.py:190
  625.5 45.8 %all-reduce = f32[64]{0:T(128)S(1)} all-reduce(f32[64]{0:T(128)S(1)} %fusion.58), channel_id=2, replica_groups=mesh['group'=32,'vocab'=16] {'group'}, use_global_device_ids=true, to_apply=%region_25.27.clone | all-reduce | flops 64 | bytes 512
  (87 shorter events, 9.9 us)
Async XLA Ops:
  7.2 401.2 %copy-start = (bf16[2,2048,196]{1,0,2:T(2,128)(2,1)S(1)}, bf16[2,2048,196]{1,0,2:T(2,128)(2,1)}, u32[]{:S(2)}) copy-start(bf16[2,2048,196]{1,0,2:T(2,128)(2,1)} %param.25) | copy-start | bytes 4816900
  7.2 104.7 %all-gather.4.cloned.1.call-start = ((), (), s32[]{:S(2)}) async-start(), calls=%async_computation.2 | async-start | bytes 3244032 | tf_op jit(solution)/shard_map/all_gather | solution.py:82
  14.7 61.9 %copy-start.10 = (s32[64]{0:T(128)S(1)}, s32[64]{0:T(128)}, u32[]{:S(2)}) copy-start(s32[64]{0:T(128)} %param.29) | copy-start | bytes 772
  14.7 62.7 %copy-start.8 = (s32[64]{0:T(128)S(1)}, s32[64]{0:T(128)}, u32[]{:S(2)}) copy-start(s32[64]{0:T(128)} %param.33) | copy-start | bytes 772
  14.7 62.7 %copy-start.9 = (s32[64]{0:T(128)S(1)}, s32[64]{0:T(128)}, u32[]{:S(2)}) copy-start(s32[64]{0:T(128)} %param.30) | copy-start | bytes 772
  15.7 55.7 %all-to-all-start = ((bf16[2,2,1,32,16,128]{5,4,1,0,2,3:T(8,128)(2,1)}), bf16[2,2,1,32,16,128]{5,4,1,0,2,3:T(8,128)(2,1)S(1)}, u32[]{:S(2)}, u32[]{:S(2)}) async-start(bf16[2,2,1,32,16,128]{5,4,1,0,2,3:T(8,128)(2,1)} %copy.63), calls=%async_computation | async-start | bytes 1048576 | tf_op jit(solution)/shard_map/all_to_all | solution.py:120
  71.4 40.3 %all-to-all-start.1 = ((bf16[2,2,1,32,16,128]{5,4,1,0,2,3:T(8,128)(2,1)}), bf16[2,2,1,32,16,128]{5,4,1,0,2,3:T(8,128)(2,1)S(1)}, u32[]{:S(2)}, u32[]{:S(2)}) async-start(bf16[2,2,1,32,16,128]{5,4,1,0,2,3:T(8,128)(2,1)} %copy.65), calls=%async_computation.1 | async-start | bytes 1048576 | tf_op jit(solution)/shard_map/all_to_all | solution.py:119
  75.8 103.8 %all-gather.6.cloned.1.call-start = ((), (), s32[]{:S(2)}) async-start(), calls=%async_computation.3 | async-start | bytes 1081344 | tf_op jit(solution)/shard_map/all_gather | solution.py:162
  76.5 219.7 %all-reduce.5.cloned.1.call-start = ((), (), s32[]{:S(2)}) async-start(), calls=%async_computation.4 | async-start | bytes 2097152 | tf_op jit(solution)/shard_map/psum | solution.py:165
  78.3 70.2 %copy-start.5 = (f32[2,128]{1,0:T(2,128)S(1)}, f32[2,128]{1,0:T(2,128)}, u32[]{:S(2)}) copy-start(f32[2,128]{1,0:T(2,128)} %param.21) | copy-start | bytes 3076
  78.4 70.2 %copy-start.6 = (f32[2,128]{1,0:T(2,128)S(1)}, f32[2,128]{1,0:T(2,128)}, u32[]{:S(2)}) copy-start(f32[2,128]{1,0:T(2,128)} %param.22) | copy-start | bytes 3076
  149.6 148.0 %copy-start.1 = (bf16[2,64,2048]{2,1,0:T(8,128)(2,1)S(1)}, bf16[2,64,2048]{2,1,0:T(8,128)(2,1)}, u32[]{:S(2)}) copy-start(bf16[2,64,2048]{2,1,0:T(8,128)(2,1)} %param.18) | copy-start | bytes 1572868
  149.6 148.0 %copy-start.2 = (f32[2,2048]{1,0:T(2,128)S(1)}, f32[2,2048]{1,0:T(2,128)}, u32[]{:S(2)}) copy-start(f32[2,2048]{1,0:T(2,128)} %param.23) | copy-start | bytes 49156
  150.2 149.0 %copy-start.3 = (f32[2,2048]{1,0:T(2,128)S(1)}, f32[2,2048]{1,0:T(2,128)}, u32[]{:S(2)}) copy-start(f32[2,2048]{1,0:T(2,128)} %param.24) | copy-start | bytes 49156
  182.4 119.8 %copy-start.4 = (s32[2048]{0:T(1024)S(1)}, s32[2048]{0:T(1024)}, u32[]{:S(2)}) copy-start(s32[2048]{0:T(1024)} %param.32) | copy-start | bytes 24580
  182.4 226.0 %all-gather.8.cloned.1.call-start = ((), (), s32[]{:S(2)}) async-start(), calls=%async_computation.5 | async-start | bytes 17301504 | tf_op jit(solution)/shard_map/all_gather | solution.py:176
  625.2 46.7 %copy-start.7 = (f32[2,64]{1,0:T(2,128)}, f32[2,64]{1,0:T(2,128)S(1)}, u32[]{:S(2)}) copy-start(f32[2,64]{1,0:T(2,128)S(1)} %fusion.54) | copy-start | bytes 1540
Sparse Core Ops, SparseCore 0:
  10.1 99.1 all-gather.3
  111.5 67.9 all-gather.5
  182.8 113.4 all-reduce.4
  300.4 107.9 all-gather.7
where the time goes:
time: 679 us; the launch traced here: 678 us
  waiting for transfers between devices  321 us (47%)
  blocking collectives  282 us (42%)
  starting transfers between devices  21.2 us (3%)
  matrix products  17.6 us (3%)
  between operations  14.8 us (2%)
  local copies, waits for them, and re-layouts  10.7 us (2%)
  other arithmetic  10.6 us (2%)
    psum x1, waiting for transfers between devices, shards(): mixed = lax.psum(partial_mix, 'vocab')  114 us
    all_gather x1, waiting for transfers between devices, shards(): lax.all_gather(final, 'group', axis=1, tiled=True)  105 us
    pmax x1, blocking collectives, shards(): peak_logit = lax.pmax(local_peak, ('group', 'vocab'))  103 us
    psum x1, blocking collectives, shards(): lax.psum((local_mass * jnp.exp(local_peak - peak_logit), local_target), (...  99.5 us
    unnamed x1, blocking collectives  45.8 us
    all_to_all x1, waiting for transfers between devices, shards(): lax.all_to_all(send_values, 'group', split_axis=3, concat_axis=3, tiled=T...  38.1 us
    psum x1, blocking collectives, shards(): lax.psum((jnp.sum(query_raw * query_raw, axis=-1), jnp.sum(key_raw * key_...  33.6 us
    all_to_all x1, waiting for transfers between devices, shards(): lax.all_to_all(send_keys, 'group', split_axis=3, concat_axis=3, tiled=True)  33.4 us
  transfers between devices with their start and end apart: 6, of which 5 were waited for; matrix products, arithmetic and copies ran while one was open for 3% of the time, Pallas kernels for 0%

commit v1 on v0

--- a/solution.py
+++ b/solution.py
@@ -182,29 +182,42 @@
     wanted = targets - first_column
     found = jnp.arange(voc_here, dtype=jnp.int32)[None, :] == wanted[:, None]
     picked = jnp.sum(jnp.where(found[None], logits, 0.0), axis=-1)
-    statistics = jnp.stack((highest, exp_sum, picked), axis=1)
-    local_peak = statistics[:, 0]
-    local_mass = statistics[:, 1]
-    local_target = statistics[:, 2]
-    peak_logit = lax.pmax(local_peak, ("group", "vocab"))
-    exp_total, target_logit = lax.psum(
-        (local_mass * jnp.exp(local_peak - peak_logit), local_target), ("group", "vocab")
-    )
+    slot_numbers = jnp.arange(request_count, dtype=jnp.int32)
+    request_of_slot = jnp.sum(
+        jnp.where(owners[None, :] == slot_numbers[:, None], slot_numbers[None, :], 0), axis=1
+    )
+    place_of_slot = jnp.sum(
+        jnp.where(deal[None, :] == request_of_slot[:, None], slot_numbers[None, :], 0), axis=1
+    )
+    group_of_slot = place_of_slot // SEQ_G
+    seq_of_slot = place_of_slot % SEQ_G
+    dest_groups = jnp.arange(groups, dtype=jnp.int32)
+    slots_per_group = request_count // groups
+    row_groups = jnp.concatenate(
+        (dest_groups[:, None], group_of_slot.reshape(groups, slots_per_group)), axis=1
+    )
+    statistics = jnp.stack((highest, exp_sum, picked), axis=0).reshape(3, 2, groups, TOK_G)
+    rows = jnp.take(statistics, row_groups.reshape(-1), axis=2).reshape(
+        3, 2, groups, 1 + slots_per_group, TOK_G
+    )
+    rows = jnp.transpose(rows, (2, 3, 0, 1, 4))
+    got = lax.all_to_all(rows, "group", split_axis=0, concat_axis=0, tiled=True)
+    peak_one = jnp.max(got[:, :, 0], axis=0)
+    mass_one = jnp.sum(got[:, :, 1] * jnp.exp(got[:, :, 0] - peak_one[None]), axis=0)
+    target_one = jnp.sum(got[:, :, 2], axis=0)
+    gathered = lax.all_gather(jnp.stack((peak_one, mass_one, target_one), axis=0), "vocab")
+    peak_logit = jnp.max(gathered[:, 0], axis=0)
+    exp_total = jnp.sum(gathered[:, 1] * jnp.exp(gathered[:, 0] - peak_logit[None]), axis=0)
+    target_logit = jnp.sum(gathered[:, 2], axis=0)
     logprobs = target_logit - (peak_logit + jnp.log(exp_total))
-    own_logprobs = lax.dynamic_slice_in_dim(logprobs, group_idx * TOK_G, TOK_G, 1)
-    gap = own_logprobs[0] - own_logprobs[1]
-    onehot_wide = onehot.astype(jnp.float32)
-    means = jnp.sum(onehot_wide * gap[:, None], axis=0) / jnp.sum(onehot_wide, axis=0)
-    slots = pick_small(owners, requests)
-    spread = jnp.sum(
-        jnp.where(
-            jnp.arange(request_count, dtype=jnp.int32)[None, :] == slots[:, None],
-            means[:, None],
-            0.0,
-        ),
-        axis=0,
-    )
-    seq_diff = lax.psum_scatter(spread, "group", scatter_dimension=0, tiled=True)
+    own_logprobs = logprobs[0]
+    my_slots = group_idx * slots_per_group + jnp.arange(slots_per_group, dtype=jnp.int32)
+    slot_groups = jnp.take(group_of_slot, my_slots)
+    slot_seqs = jnp.take(seq_of_slot, my_slots)
+    slot_ids = jnp.take(segment_ids, slot_groups, axis=0)
+    in_seq = (slot_ids == slot_seqs[:, None]).astype(jnp.float32)
+    slot_gap = logprobs[1:, 0] - logprobs[1:, 1]
+    seq_diff = jnp.sum(in_seq * slot_gap, axis=1) / jnp.sum(in_seq, axis=1)
     return (hidden_out, own_logprobs, seq_diff)
 
 

time: 679 us -> 486 us (0.72)
  blocking collectives: 282 us -> 52.1 us
  waiting for transfers between devices: 321 us -> 338 us
  starting transfers between devices: 21.2 us -> 30.2 us
    pmax x1 -> x0, blocking collectives: 103 us -> none  [shards(): peak_logit = lax.pmax(local_peak, ('group', 'vocab'))]
    psum x1 -> x0, blocking collectives: 99.5 us -> none  [shards(): lax.psum((local_mass * jnp.exp(local_peak - peak_logit), local_target), (...]
    unnamed x1 -> x0, blocking collectives: 45.8 us -> none
    all_gather x0 -> x1, blocking collectives: none -> 18.6 us  [shards(): lax.all_gather(jnp.stack((peak_one, mass_one, target_one), axis=0), 'vocab')]
    all_to_all x0 -> x1, waiting for transfers between devices: none -> 15.2 us  [shards(): got = lax.all_to_all(rows, 'group', split_axis=0, concat_axis=0, tiled=True)]
    all_to_all x0 -> x1, starting transfers between devices: none -> 9.15 us  [shards(): got = lax.all_to_all(rows, 'group', split_axis=0, concat_axis=0, tiled=True)]
  transfers between devices with their start and end apart: 6 -> 7, of which waited for: 5 -> 6; matrix products, arithmetic and copies ran while one was open for 3% -> 4% of each run, Pallas kernels for 0% -> 0%
where the time goes in v1:
time: 486 us; the launch traced here: 480 us
  waiting for transfers between devices  338 us (70%)
  blocking collectives  52.1 us (11%)
  starting transfers between devices  30.2 us (6%)
  matrix products  17.6 us (4%)
  other arithmetic  14.4 us (3%)
  between operations  14.3 us (3%)
  local copies, waits for them, and re-layouts  13.9 us (3%)
    psum x1, waiting for transfers between devices, shards(): mixed = lax.psum(partial_mix, 'vocab')  114 us
    all_gather x1, waiting for transfers between devices, shards(): lax.all_gather(final, 'group', axis=1, tiled=True)  106 us
    all_to_all x1, waiting for transfers between devices, shards(): lax.all_to_all(send_values, 'group', split_axis=3, concat_axis=3, tiled=T...  37.1 us
    all_to_all x1, waiting for transfers between devices, shards(): lax.all_to_all(send_keys, 'group', split_axis=3, concat_axis=3, tiled=True)  35.2 us
    psum x1, blocking collectives, shards(): lax.psum((jnp.sum(query_raw * query_raw, axis=-1), jnp.sum(key_raw * key_...  33.5 us
    all_gather x1, waiting for transfers between devices, shards(): lax.all_gather(out_weight, 'group', axis=2, tiled=True)  28.7 us
    all_gather x1, blocking collectives, shards(): lax.all_gather(jnp.stack((peak_one, mass_one, target_one), axis=0), 'vocab')  18.6 us
    all_to_all x1, starting transfers between devices, shards(): lax.all_to_all(send_values, 'group', split_axis=3, concat_axis=3, tiled=T...  16.7 us
  transfers between devices with their start and end apart: 7, of which 6 were waited for; matrix products, arithmetic and copies ran while one was open for 4% of the time, Pallas kernels for 0%

profile of v1, /device:TPU:1, one launch (start us, length us, event | category | flops | bytes accessed | tf_op | source)
XLA Modules:
  0.0 480.0 jit_solution(10969792266517711553)
XLA Ops:
  12.8 1.7 gather_fusion.4
  14.5 1.7 gather_fusion.3
  17.4 16.7 %all-to-all-start = ((bf16[2,2,1,32,16,128]{5,4,1,0,2,3:T(8,128)(2,1)}), bf16[2,2,1,32,16,128]{5,4,1,0,2,3:T(8,128)(2,1)S(1)}, u32[]{:S(2)}, u32[]{:S(2)}) async-start(bf16[2,2,1,32,16,128]{5,4,1,0,2,3:T(8,128)(2,1)} %copy.104), calls=%async_computation | async-start | bytes 1048576 | tf_op jit(solution)/shard_map/all_to_all | solution.py:120
  34.1 0.9 copy.106
  35.0 37.1 %all-to-all-done = bf16[2,2,1,32,16,128]{5,4,1,0,2,3:T(8,128)(2,1)S(1)} async-done(((bf16[2,2,1,32,16,128]{5,4,1,0,2,3:T(8,128)(2,1)}), bf16[2,2,1,32,16,128]{5,4,1,0,2,3:T(8,128)(2,1)S(1)}, u32[]{:S(2)}, u32[]{:S(2)}) %all-to-all-start) | async-done | bytes 524320 | tf_op jit(solution)/shard_map/all_to_all | solution.py:120
  72.1 4.2 all-to-all-start.1
  78.2 35.2 %all-to-all-done.1 = bf16[2,2,1,32,16,128]{5,4,1,0,2,3:T(8,128)(2,1)S(1)} async-done(((bf16[2,2,1,32,16,128]{5,4,1,0,2,3:T(8,128)(2,1)}), bf16[2,2,1,32,16,128]{5,4,1,0,2,3:T(8,128)(2,1)S(1)}, u32[]{:S(2)}, u32[]{:S(2)}) %all-to-all-start.1) | async-done | bytes 524320 | tf_op jit(solution)/shard_map/all_to_all | solution.py:119
  113.4 2.6 fusion.76
  116.5 33.5 %all-reduce = (f32[2,64]{1,0:T(2,128)S(1)}, f32[2,64]{1,0:T(2,128)S(1)}) all-reduce(f32[2,64]{1,0:T(2,128)S(1)} %get-tuple-element.43, f32[2,64]{1,0:T(2,128)S(1)} %get-tuple-element.44), channel_id=1, replica_groups=mesh['group'=32,'vocab'=16] {'vocab'}, use_global_device_ids=true, to_apply=%region_2.4 | all-reduce | flops 256 | bytes 2048 | tf_op jit(solution)/shard_map/psum | solution.py:88
  151.7 28.7 %all-gather.7.cloned.1.call-done = bf16[2,128,2048]{1,2,0:T(8,128)(2,1)} async-done(((bf16[2,128,64]{1,2,0:T(8,128)(2,1)}), bf16[2,128,2048]{1,2,0:T(8,128)(2,1)}) %all-gather.7.cloned.1.call-update) | async-done | bytes 1048592 | tf_op jit(solution)/shard_map/all_gather | solution.py:162
  180.4 2.9 fusion.15
  183.4 113.8 %all-reduce.3.cloned.1.call-done = f32[2,64,2048]{2,1,0:T(8,128)} async-done(((f32[2,64,2048]{2,1,0:T(8,128)}), f32[2,64,2048]{2,1,0:T(8,128)}) %all-reduce.3.cloned.1.call-update) | async-done | bytes 1048592 | tf_op jit(solution)/shard_map/psum | solution.py:165
  297.1 1.4 multiply_reduce_fusion
  298.5 1.6 fusion.12
  300.2 1.0 fusion.14
  303.1 106.2 %all-gather.9.cloned.1.call-done = bf16[2,2048,2048]{2,1,0:T(8,128)(2,1)} async-done(((bf16[2,64,2048]{2,1,0:T(8,128)(2,1)}), bf16[2,2048,2048]{2,1,0:T(8,128)(2,1)}) %all-gather.9.cloned.1.call-update) | async-done | bytes 16777232 | tf_op jit(solution)/shard_map/all_gather | solution.py:176
  409.3 11.1 %fusion.75 = (f32[2,2048]{1,0:T(2,128)S(1)}, f32[2,2048,196]{1,2,0:T(8,128)}) fusion(bf16[2,2048,2048]{2,1,0:T(8,128)(2,1)} %all-gather.9.cloned.1.call-done, bf16[2,2048,196]{1,0,2:T(2,128)(2,1)S(1)} %copy-done), kind=kOutput, calls=%fused_computation.172 | convolution fusion | flops 3289133056 | bytes 21610496 | tf_op jit(solution)/shard_map/mtd,mdv->mtv/dot_general | solution.py:174
  420.5 2.8 exponential_reduce_fusion
  423.6 1.0 gather_fusion.1
  424.9 0.9 reshape.540
  425.9 9.1 %all-to-all-start.2 = ((f32[32,1,1152]{2,1,0:T(1,128)}), f32[32,1,1152]{2,1,0:T(1,128)S(1)}, u32[]{:S(2)}, u32[]{:S(2)}) async-start(f32[32,1,1152]{2,1,0:T(1,128)} %reshape.540), calls=%async_computation.2 | async-start | bytes 294912 | tf_op jit(solution)/shard_map/all_to_all | solution.py:204
  436.3 15.2 %all-to-all-done.2 = f32[32,1,1152]{2,1,0:T(1,128)S(1)} async-done(((f32[32,1,1152]{2,1,0:T(1,128)}), f32[32,1,1152]{2,1,0:T(1,128)S(1)}, u32[]{:S(2)}, u32[]{:S(2)}) %all-to-all-start.2) | async-done | bytes 147488 | tf_op jit(solution)/shard_map/all_to_all | solution.py:204
  452.0 1.0 reduce.8
  453.5 18.6 %all-gather = f32[48,3,2,64]{3,2,1,0:T(2,128)S(1)} all-gather(f32[3,3,2,64]{3,2,1,0:T(2,128)S(1)} %pad_maximum_fusion.3), channel_id=2, replica_groups=mesh['group'=32,'vocab'=16] {'vocab'}, dimensions={0}, use_global_device_ids=true | all-gather | bytes 78336 | tf_op jit(solution)/shard_map/all_gather | solution.py:208
  (120 shorter events, 16.8 us)
Async XLA Ops:
  7.2 402.1 %copy-start = (bf16[2,2048,196]{1,0,2:T(2,128)(2,1)S(1)}, bf16[2,2048,196]{1,0,2:T(2,128)(2,1)}, u32[]{:S(2)}) copy-start(bf16[2,2048,196]{1,0,2:T(2,128)(2,1)} %param.27) | copy-start | bytes 4816900
  7.2 106.2 %all-gather.5.cloned.1.call-start = ((), (), s32[]{:S(2)}) async-start(), calls=%async_computation.3 | async-start | bytes 3244032 | tf_op jit(solution)/shard_map/all_gather | solution.py:82
  16.3 60.8 %copy-start.8 = (s32[64]{0:T(128)S(1)}, s32[64]{0:T(128)}, u32[]{:S(2)}) copy-start(s32[64]{0:T(128)} %param.31) | copy-start | bytes 772
  16.3 60.9 %copy-start.7 = (s32[32,64]{1,0:T(8,128)S(1)}, s32[32,64]{1,0:T(8,128)}, u32[]{:S(2)}) copy-start(s32[32,64]{1,0:T(8,128)} %param.33) | copy-start | bytes 24580
  16.3 60.9 %copy-start.9 = (s32[64]{0:T(128)S(1)}, s32[64]{0:T(128)}, u32[]{:S(2)}) copy-start(s32[64]{0:T(128)} %param.32) | copy-start | bytes 772
  17.4 54.7 %all-to-all-start = ((bf16[2,2,1,32,16,128]{5,4,1,0,2,3:T(8,128)(2,1)}), bf16[2,2,1,32,16,128]{5,4,1,0,2,3:T(8,128)(2,1)S(1)}, u32[]{:S(2)}, u32[]{:S(2)}) async-start(bf16[2,2,1,32,16,128]{5,4,1,0,2,3:T(8,128)(2,1)} %copy.104), calls=%async_computation | async-start | bytes 1048576 | tf_op jit(solution)/shard_map/all_to_all | solution.py:120
  72.1 41.3 %all-to-all-start.1 = ((bf16[2,2,1,32,16,128]{5,4,1,0,2,3:T(8,128)(2,1)}), bf16[2,2,1,32,16,128]{5,4,1,0,2,3:T(8,128)(2,1)S(1)}, u32[]{:S(2)}, u32[]{:S(2)}) async-start(bf16[2,2,1,32,16,128]{5,4,1,0,2,3:T(8,128)(2,1)} %copy.106), calls=%async_computation.1 | async-start | bytes 1048576 | tf_op jit(solution)/shard_map/all_to_all | solution.py:119
  76.3 104.1 %all-gather.7.cloned.1.call-start = ((), (), s32[]{:S(2)}) async-start(), calls=%async_computation.4 | async-start | bytes 1081344 | tf_op jit(solution)/shard_map/all_gather | solution.py:162
  77.0 220.1 %all-reduce.3.cloned.1.call-start = ((), (), s32[]{:S(2)}) async-start(), calls=%async_computation.5 | async-start | bytes 2097152 | tf_op jit(solution)/shard_map/psum | solution.py:165
  78.1 71.9 %copy-start.5 = (f32[2,128]{1,0:T(2,128)S(1)}, f32[2,128]{1,0:T(2,128)}, u32[]{:S(2)}) copy-start(f32[2,128]{1,0:T(2,128)} %param.23) | copy-start | bytes 3076
  78.2 71.9 %copy-start.6 = (f32[2,128]{1,0:T(2,128)S(1)}, f32[2,128]{1,0:T(2,128)}, u32[]{:S(2)}) copy-start(f32[2,128]{1,0:T(2,128)} %param.24) | copy-start | bytes 3076
  151.1 147.4 %copy-start.1 = (bf16[2,64,2048]{2,1,0:T(8,128)(2,1)S(1)}, bf16[2,64,2048]{2,1,0:T(8,128)(2,1)}, u32[]{:S(2)}) copy-start(bf16[2,64,2048]{2,1,0:T(8,128)(2,1)} %param.20) | copy-start | bytes 1572868
  151.1 147.4 %copy-start.2 = (f32[2,2048]{1,0:T(2,128)S(1)}, f32[2,2048]{1,0:T(2,128)}, u32[]{:S(2)}) copy-start(f32[2,2048]{1,0:T(2,128)} %param.25) | copy-start | bytes 49156
  151.7 148.4 %copy-start.3 = (f32[2,2048]{1,0:T(2,128)S(1)}, f32[2,2048]{1,0:T(2,128)}, u32[]{:S(2)}) copy-start(f32[2,2048]{1,0:T(2,128)} %param.26) | copy-start | bytes 49156
  183.3 119.5 %copy-start.4 = (s32[2048]{0:T(1024)S(1)}, s32[2048]{0:T(1024)}, u32[]{:S(2)}) copy-start(s32[2048]{0:T(1024)} %param.34) | copy-start | bytes 24580
  183.3 226.0 %all-gather.9.cloned.1.call-start = ((), (), s32[]{:S(2)}) async-start(), calls=%async_computation.6 | async-start | bytes 17301504 | tf_op jit(solution)/shard_map/all_gather | solution.py:176
  425.9 25.6 %all-to-all-start.2 = ((f32[32,1,1152]{2,1,0:T(1,128)}), f32[32,1,1152]{2,1,0:T(1,128)S(1)}, u32[]{:S(2)}, u32[]{:S(2)}) async-start(f32[32,1,1152]{2,1,0:T(1,128)} %reshape.540), calls=%async_computation.2 | async-start | bytes 294912 | tf_op jit(solution)/shard_map/all_to_all | solution.py:204
Sparse Core Ops, SparseCore 0:
  10.1 98.9 all-gather.4
  111.3 69.1 all-gather.6
  183.7 113.4 all-reduce.2
  301.3 107.9 all-gather.8

commit v2 on v1

--- a/solution.py
+++ b/solution.py
@@ -162,7 +162,7 @@
         lax.all_gather(out_weight, "group", axis=2, tiled=True),
         preferred_element_type=jnp.float32,
     )
-    mixed = lax.psum(partial_mix, "vocab")
+    mixed = lax.psum(partial_mix.astype(jnp.bfloat16), "vocab").astype(jnp.float32)
     hidden_new = (hidden_in.astype(jnp.float32) + rms_scale(mixed, post_gain[:, None, :])).astype(
         jnp.bfloat16
     )

time: 486 us -> 484 us (level)
  no operation moved by 1% of the time
where the time goes in v2:
time: 484 us; the launch traced here: 478 us
  waiting for transfers between devices  336 us (69%)
  blocking collectives  52 us (11%)
  starting transfers between devices  30.2 us (6%)
  matrix products  17.4 us (4%)
  local copies, waits for them, and re-layouts  14.5 us (3%)
  between operations  14.3 us (3%)
  other arithmetic  14.2 us (3%)
    psum x1, waiting for transfers between devices, shards(): lax.psum(partial_mix.astype(jnp.bfloat16), 'vocab').astype(jnp.float32)  112 us
    all_gather x1, waiting for transfers between devices, shards(): lax.all_gather(final, 'group', axis=1, tiled=True)  107 us
    all_to_all x1, waiting for transfers between devices, shards(): lax.all_to_all(send_values, 'group', split_axis=3, concat_axis=3, tiled=T...  37.2 us
    all_to_all x1, waiting for transfers between devices, shards(): lax.all_to_all(send_keys, 'group', split_axis=3, concat_axis=3, tiled=True)  34.4 us
    psum x1, blocking collectives, shards(): lax.psum((jnp.sum(query_raw * query_raw, axis=-1), jnp.sum(key_raw * key_...  33.4 us
    all_gather x1, waiting for transfers between devices, shards(): lax.all_gather(out_weight, 'group', axis=2, tiled=True)  28.9 us
    all_gather x1, blocking collectives, shards(): lax.all_gather(jnp.stack((peak_one, mass_one, target_one), axis=0), 'vocab')  18.6 us
    all_to_all x1, starting transfers between devices, shards(): lax.all_to_all(send_values, 'group', split_axis=3, concat_axis=3, tiled=T...  16.7 us
  transfers between devices with their start and end apart: 7, of which 6 were waited for; matrix products, arithmetic and copies ran while one was open for 4% of the time, Pallas kernels for 0%

profile of v2, /device:TPU:1, one launch (start us, length us, event | category | flops | bytes accessed | tf_op | source)
XLA Modules:
  0.0 478.3 jit_solution(5334523621066422826)
XLA Ops:
  12.8 1.7 gather_fusion.4
  14.5 1.7 gather_fusion.3
  17.3 16.7 %all-to-all-start = ((bf16[2,2,1,32,16,128]{5,4,1,0,2,3:T(8,128)(2,1)}), bf16[2,2,1,32,16,128]{5,4,1,0,2,3:T(8,128)(2,1)S(1)}, u32[]{:S(2)}, u32[]{:S(2)}) async-start(bf16[2,2,1,32,16,128]{5,4,1,0,2,3:T(8,128)(2,1)} %copy.104), calls=%async_computation | async-start | bytes 1048576 | tf_op jit(solution)/shard_map/all_to_all | solution.py:120
  34.1 0.9 copy.106
  35.0 37.2 %all-to-all-done = bf16[2,2,1,32,16,128]{5,4,1,0,2,3:T(8,128)(2,1)S(1)} async-done(((bf16[2,2,1,32,16,128]{5,4,1,0,2,3:T(8,128)(2,1)}), bf16[2,2,1,32,16,128]{5,4,1,0,2,3:T(8,128)(2,1)S(1)}, u32[]{:S(2)}, u32[]{:S(2)}) %all-to-all-start) | async-done | bytes 524320 | tf_op jit(solution)/shard_map/all_to_all | solution.py:120
  72.1 4.2 all-to-all-start.1
  78.9 34.4 %all-to-all-done.1 = bf16[2,2,1,32,16,128]{5,4,1,0,2,3:T(8,128)(2,1)S(1)} async-done(((bf16[2,2,1,32,16,128]{5,4,1,0,2,3:T(8,128)(2,1)}), bf16[2,2,1,32,16,128]{5,4,1,0,2,3:T(8,128)(2,1)S(1)}, u32[]{:S(2)}, u32[]{:S(2)}) %all-to-all-start.1) | async-done | bytes 524320 | tf_op jit(solution)/shard_map/all_to_all | solution.py:119
  113.3 2.6 fusion.80
  116.4 33.4 %all-reduce = (f32[2,64]{1,0:T(2,128)S(1)}, f32[2,64]{1,0:T(2,128)S(1)}) all-reduce(f32[2,64]{1,0:T(2,128)S(1)} %get-tuple-element.43, f32[2,64]{1,0:T(2,128)S(1)} %get-tuple-element.44), channel_id=1, replica_groups=mesh['group'=32,'vocab'=16] {'vocab'}, use_global_device_ids=true, to_apply=%region_2.4 | all-reduce | flops 256 | bytes 2048 | tf_op jit(solution)/shard_map/psum | solution.py:88
  151.6 28.9 %all-gather.7.cloned.1.call-done = bf16[2,128,2048]{1,2,0:T(8,128)(2,1)} async-done(((bf16[2,128,64]{1,2,0:T(8,128)(2,1)}), bf16[2,128,2048]{1,2,0:T(8,128)(2,1)}) %all-gather.7.cloned.1.call-update) | async-done | bytes 1048592 | tf_op jit(solution)/shard_map/all_gather | solution.py:162
  180.5 2.7 convolution_convert_fusion
  183.2 111.7 %all-reduce.3.cloned.1.call-done = bf16[2,64,2048]{2,1,0:T(8,128)(2,1)} async-done(((bf16[2,64,2048]{2,1,0:T(8,128)(2,1)}), bf16[2,64,2048]{2,1,0:T(8,128)(2,1)}) %all-reduce.3.cloned.1.call-update) | async-done | bytes 524304 | tf_op jit(solution)/shard_map/psum | solution.py:165
  295.0 1.2 fusion.12
  296.2 1.5 fusion.16
  297.7 1.0 fusion.18
  300.6 106.9 %all-gather.9.cloned.1.call-done = bf16[2,2048,2048]{2,1,0:T(8,128)(2,1)} async-done(((bf16[2,64,2048]{2,1,0:T(8,128)(2,1)}), bf16[2,2048,2048]{2,1,0:T(8,128)(2,1)}) %all-gather.9.cloned.1.call-update) | async-done | bytes 16777232 | tf_op jit(solution)/shard_map/all_gather | solution.py:176
  407.5 11.1 %fusion.79 = (f32[2,2048]{1,0:T(2,128)S(1)}, f32[2,2048,196]{1,2,0:T(8,128)}) fusion(bf16[2,2048,2048]{2,1,0:T(8,128)(2,1)} %all-gather.9.cloned.1.call-done, bf16[2,2048,196]{1,0,2:T(2,128)(2,1)S(1)} %copy-done), kind=kOutput, calls=%fused_computation.176 | convolution fusion | flops 3289133056 | bytes 21610496 | tf_op jit(solution)/shard_map/mtd,mdv->mtv/dot_general | solution.py:174
  418.8 2.8 exponential_reduce_fusion
  421.9 1.0 gather_fusion.1
  423.2 0.9 reshape.540
  424.1 9.2 %all-to-all-start.2 = ((f32[32,1,1152]{2,1,0:T(1,128)}), f32[32,1,1152]{2,1,0:T(1,128)S(1)}, u32[]{:S(2)}, u32[]{:S(2)}) async-start(f32[32,1,1152]{2,1,0:T(1,128)} %reshape.540), calls=%async_computation.2 | async-start | bytes 294912 | tf_op jit(solution)/shard_map/all_to_all | solution.py:204
  434.5 15.2 %all-to-all-done.2 = f32[32,1,1152]{2,1,0:T(1,128)S(1)} async-done(((f32[32,1,1152]{2,1,0:T(1,128)}), f32[32,1,1152]{2,1,0:T(1,128)S(1)}, u32[]{:S(2)}, u32[]{:S(2)}) %all-to-all-start.2) | async-done | bytes 147488 | tf_op jit(solution)/shard_map/all_to_all | solution.py:204
  450.2 1.0 reduce.8
  451.7 18.6 %all-gather = f32[48,3,2,64]{3,2,1,0:T(2,128)S(1)} all-gather(f32[3,3,2,64]{3,2,1,0:T(2,128)S(1)} %pad_maximum_fusion.3), channel_id=2, replica_groups=mesh['group'=32,'vocab'=16] {'vocab'}, dimensions={0}, use_global_device_ids=true | all-gather | bytes 78336 | tf_op jit(solution)/shard_map/all_gather | solution.py:208
  (120 shorter events, 17.5 us)
Async XLA Ops:
  7.2 400.4 %copy-start = (bf16[2,2048,196]{1,0,2:T(2,128)(2,1)S(1)}, bf16[2,2048,196]{1,0,2:T(2,128)(2,1)}, u32[]{:S(2)}) copy-start(bf16[2,2048,196]{1,0,2:T(2,128)(2,1)} %param.27) | copy-start | bytes 4816900
  7.2 106.1 %all-gather.5.cloned.1.call-start = ((), (), s32[]{:S(2)}) async-start(), calls=%async_computation.3 | async-start | bytes 3244032 | tf_op jit(solution)/shard_map/all_gather | solution.py:82
  16.3 60.8 %copy-start.8 = (s32[64]{0:T(128)S(1)}, s32[64]{0:T(128)}, u32[]{:S(2)}) copy-start(s32[64]{0:T(128)} %param.31) | copy-start | bytes 772
  16.3 61.6 %copy-start.9 = (s32[64]{0:T(128)S(1)}, s32[64]{0:T(128)}, u32[]{:S(2)}) copy-start(s32[64]{0:T(128)} %param.32) | copy-start | bytes 772
  17.3 54.8 %all-to-all-start = ((bf16[2,2,1,32,16,128]{5,4,1,0,2,3:T(8,128)(2,1)}), bf16[2,2,1,32,16,128]{5,4,1,0,2,3:T(8,128)(2,1)S(1)}, u32[]{:S(2)}, u32[]{:S(2)}) async-start(bf16[2,2,1,32,16,128]{5,4,1,0,2,3:T(8,128)(2,1)} %copy.104), calls=%async_computation | async-start | bytes 1048576 | tf_op jit(solution)/shard_map/all_to_all | solution.py:120
  72.1 41.2 %all-to-all-start.1 = ((bf16[2,2,1,32,16,128]{5,4,1,0,2,3:T(8,128)(2,1)}), bf16[2,2,1,32,16,128]{5,4,1,0,2,3:T(8,128)(2,1)S(1)}, u32[]{:S(2)}, u32[]{:S(2)}) async-start(bf16[2,2,1,32,16,128]{5,4,1,0,2,3:T(8,128)(2,1)} %copy.106), calls=%async_computation.1 | async-start | bytes 1048576 | tf_op jit(solution)/shard_map/all_to_all | solution.py:119
  76.3 104.2 %all-gather.7.cloned.1.call-start = ((), (), s32[]{:S(2)}) async-start(), calls=%async_computation.4 | async-start | bytes 1081344 | tf_op jit(solution)/shard_map/all_gather | solution.py:162
  77.0 217.9 %all-reduce.3.cloned.1.call-start = ((), (), s32[]{:S(2)}) async-start(), calls=%async_computation.5 | async-start | bytes 1048576 | tf_op jit(solution)/shard_map/psum | solution.py:165
  78.8 71.1 %copy-start.5 = (f32[2,128]{1,0:T(2,128)S(1)}, f32[2,128]{1,0:T(2,128)}, u32[]{:S(2)}) copy-start(f32[2,128]{1,0:T(2,128)} %param.23) | copy-start | bytes 3076
  78.8 71.1 %copy-start.6 = (f32[2,128]{1,0:T(2,128)S(1)}, f32[2,128]{1,0:T(2,128)}, u32[]{:S(2)}) copy-start(f32[2,128]{1,0:T(2,128)} %param.24) | copy-start | bytes 3076
  150.2 146.0 %copy-start.1 = (bf16[2,64,2048]{2,1,0:T(8,128)(2,1)S(1)}, bf16[2,64,2048]{2,1,0:T(8,128)(2,1)}, u32[]{:S(2)}) copy-start(bf16[2,64,2048]{2,1,0:T(8,128)(2,1)} %param.20) | copy-start | bytes 1572868
  150.2 146.0 %copy-start.2 = (f32[2,2048]{1,0:T(2,128)S(1)}, f32[2,2048]{1,0:T(2,128)}, u32[]{:S(2)}) copy-start(f32[2,2048]{1,0:T(2,128)} %param.25) | copy-start | bytes 49156
  151.0 146.7 %copy-start.3 = (f32[2,2048]{1,0:T(2,128)S(1)}, f32[2,2048]{1,0:T(2,128)}, u32[]{:S(2)}) copy-start(f32[2,2048]{1,0:T(2,128)} %param.26) | copy-start | bytes 49156
  180.5 119.9 %copy-start.4 = (s32[2048]{0:T(1024)S(1)}, s32[2048]{0:T(1024)}, u32[]{:S(2)}) copy-start(s32[2048]{0:T(1024)} %param.34) | copy-start | bytes 24580
  183.2 224.3 %all-gather.9.cloned.1.call-start = ((), (), s32[]{:S(2)}) async-start(), calls=%async_computation.6 | async-start | bytes 17301504 | tf_op jit(solution)/shard_map/all_gather | solution.py:176
  418.8 14.6 %copy-start.7 = (s32[32,64]{1,0:T(8,128)S(1)}, s32[32,64]{1,0:T(8,128)}, u32[]{:S(2)}) copy-start(s32[32,64]{1,0:T(8,128)} %param.33) | copy-start | bytes 24580
  424.1 25.6 %all-to-all-start.2 = ((f32[32,1,1152]{2,1,0:T(1,128)}), f32[32,1,1152]{2,1,0:T(1,128)S(1)}, u32[]{:S(2)}, u32[]{:S(2)}) async-start(f32[32,1,1152]{2,1,0:T(1,128)} %reshape.540), calls=%async_computation.2 | async-start | bytes 294912 | tf_op jit(solution)/shard_map/all_to_all | solution.py:204
Sparse Core Ops, SparseCore 0:
  10.1 99.1 all-gather.4
  111.5 68.9 all-gather.6
  183.7 111.2 all-reduce.2
  298.8 108.6 all-gather.8

commit v3 on v2

--- a/solution.py
+++ b/solution.py
@@ -76,12 +76,9 @@
     heads_dev = HEADS // vocab_count
     score_scale = 1.0 / math.sqrt(head_size)
     request_count = deal.shape[0]
-    united = jnp.einsum(
-        "mtd,mdc->mtc",
-        hidden_in,
-        lax.all_gather(qkv_weight, "group", axis=1, tiled=True),
-        preferred_element_type=jnp.float32,
-    )
+    qkv_rows = lax.all_gather(qkv_weight, "group", axis=1, tiled=True)
+    qkv_rows, out_weight = lax.optimization_barrier((qkv_rows, out_weight))
+    united = jnp.einsum("mtd,mdc->mtc", hidden_in, qkv_rows, preferred_element_type=jnp.float32)
     united = united.reshape(2, TOK_G, heads_dev, 3, head_size)
     query_raw = united[:, :, :, 0, :].reshape(2, TOK_G, heads_dev * head_size)
     key_raw = united[:, :, :, 1, :].reshape(2, TOK_G, heads_dev * head_size)
@@ -156,17 +153,21 @@
         .reshape(2, TOK_G, heads_dev * head_size)
         .astype(jnp.bfloat16)
     )
-    partial_mix = jnp.einsum(
-        "mtc,mcd->mtd",
-        attended,
-        lax.all_gather(out_weight, "group", axis=2, tiled=True),
-        preferred_element_type=jnp.float32,
-    )
-    mixed = lax.psum(partial_mix.astype(jnp.bfloat16), "vocab").astype(jnp.float32)
+    col_width = D // vocab_count
+    head_rows = lax.all_gather(out_weight, "group", axis=2, tiled=True)
+    head_rows = jnp.transpose(
+        head_rows.reshape(2, heads_dev * head_size, vocab_count, col_width), (2, 0, 1, 3)
+    )
+    column_block = lax.all_to_all(head_rows, "vocab", split_axis=0, concat_axis=0, tiled=True)
+    column_block = jnp.transpose(column_block, (1, 0, 2, 3)).reshape(2, D, col_width)
+    attended_all = lax.all_gather(attended, "vocab", axis=2, tiled=True)
+    mixed_block = jnp.einsum(
+        "mtc,mcd->mtd", attended_all, column_block, preferred_element_type=jnp.float32
+    )
+    mixed = lax.all_gather(mixed_block, "vocab", axis=2, tiled=True)
     hidden_new = (hidden_in.astype(jnp.float32) + rms_scale(mixed, post_gain[:, None, :])).astype(
         jnp.bfloat16
     )
-    col_width = D // vocab_count
     hidden_out = lax.dynamic_slice_in_dim(hidden_new, vocab_idx * col_width, col_width, 2)
     final = rms_scale(hidden_new.astype(jnp.float32), final_gain[:, None, :]).astype(jnp.bfloat16)
     voc_here = head_weight.shape[2]

time: 484 us -> 465 us (0.961)
  waiting for transfers between devices: 336 us -> 281 us
  blocking collectives: 52 us -> 76.7 us
  starting transfers between devices: 30.2 us -> 36.7 us
    psum x1 -> x0, waiting for transfers between devices: 112 us -> none  [shards(): lax.psum(partial_mix.astype(jnp.bfloat16), 'vocab').astype(jnp.float32)]
    all_gather x2 -> x3, waiting for transfers between devices: 28.9 us -> 85.4 us  [the longest x1 56.9 us: shards(): mixed = lax.all_gather(mixed_block, 'vocab', axis=2, tiled=True)]
    all_gather x0 -> x1, blocking collectives: none -> 24.7 us  [shards(): attended_all = lax.all_gather(attended, 'vocab', axis=2, tiled=True)]
    all_to_all x0 -> x1, starting transfers between devices: none -> 6.52 us  [shards(): lax.all_to_all(head_rows, 'vocab', split_axis=0, concat_axis=0, tiled=True)]
  transfers between devices with their start and end apart: 7 -> 8, of which waited for: 6 -> 6; matrix products, arithmetic and copies ran while one was open for 4% -> 5% of each run, Pallas kernels for 0% -> 0%
where the time goes in v3:
time: 465 us; the launch traced here: 459 us
  waiting for transfers between devices  281 us (60%)
  blocking collectives  76.7 us (16%)
  starting transfers between devices  36.7 us (8%)
  matrix products  18.4 us (4%)
  local copies, waits for them, and re-layouts  17 us (4%)
  other arithmetic  15.4 us (3%)
  between operations  14.3 us (3%)
    all_gather x1, waiting for transfers between devices, shards(): lax.all_gather(final, 'group', axis=1, tiled=True)  106 us
    all_gather x1, waiting for transfers between devices, shards(): mixed = lax.all_gather(mixed_block, 'vocab', axis=2, tiled=True)  56.9 us
    all_to_all x1, waiting for transfers between devices, shards(): lax.all_to_all(send_values, 'group', split_axis=3, concat_axis=3, tiled=T...  37 us
    all_to_all x1, waiting for transfers between devices, shards(): lax.all_to_all(send_keys, 'group', split_axis=3, concat_axis=3, tiled=True)  35.8 us
    psum x1, blocking collectives, shards(): lax.psum((jnp.sum(query_raw * query_raw, axis=-1), jnp.sum(key_raw * key_...  33.4 us
    all_gather x1, waiting for transfers between devices, shards(): head_rows = lax.all_gather(out_weight, 'group', axis=2, tiled=True)  28.5 us
    all_gather x1, blocking collectives, shards(): attended_all = lax.all_gather(attended, 'vocab', axis=2, tiled=True)  24.7 us
    all_gather x1, blocking collectives, shards(): lax.all_gather(jnp.stack((peak_one, mass_one, target_one), axis=0), 'vocab')  18.6 us
  transfers between devices with their start and end apart: 8, of which 6 were waited for; matrix products, arithmetic and copies ran while one was open for 5% of the time, Pallas kernels for 0%

profile of v3, /device:TPU:1, one launch (start us, length us, event | category | flops | bytes accessed | tf_op | source)
XLA Modules:
  0.0 459.0 jit_solution(9521030148432320791)
XLA Ops:
  12.8 1.7 gather_fusion.4
  14.5 1.7 gather_fusion.3
  17.4 16.7 %all-to-all-start = ((bf16[2,2,1,32,16,128]{5,4,1,0,2,3:T(8,128)(2,1)}), bf16[2,2,1,32,16,128]{5,4,1,0,2,3:T(8,128)(2,1)S(1)}, u32[]{:S(2)}, u32[]{:S(2)}) async-start(bf16[2,2,1,32,16,128]{5,4,1,0,2,3:T(8,128)(2,1)} %copy.110), calls=%async_computation | async-start | bytes 1048576 | tf_op jit(solution)/shard_map/all_to_all | solution.py:117
  35.0 37.0 %all-to-all-done = bf16[2,2,1,32,16,128]{5,4,1,0,2,3:T(8,128)(2,1)S(1)} async-done(((bf16[2,2,1,32,16,128]{5,4,1,0,2,3:T(8,128)(2,1)}), bf16[2,2,1,32,16,128]{5,4,1,0,2,3:T(8,128)(2,1)S(1)}, u32[]{:S(2)}, u32[]{:S(2)}) %all-to-all-start) | async-done | bytes 524320 | tf_op jit(solution)/shard_map/all_to_all | solution.py:117
  72.0 4.2 all-to-all-start.1
  78.1 35.8 %all-to-all-done.1 = bf16[2,2,1,32,16,128]{5,4,1,0,2,3:T(8,128)(2,1)S(1)} async-done(((bf16[2,2,1,32,16,128]{5,4,1,0,2,3:T(8,128)(2,1)}), bf16[2,2,1,32,16,128]{5,4,1,0,2,3:T(8,128)(2,1)S(1)}, u32[]{:S(2)}, u32[]{:S(2)}) %all-to-all-start.1) | async-done | bytes 524320 | tf_op jit(solution)/shard_map/all_to_all | solution.py:116
  113.9 2.6 convolution_bitcast_fusion
  116.9 33.4 %all-reduce = (f32[2,64]{1,0:T(2,128)S(1)}, f32[2,64]{1,0:T(2,128)S(1)}) all-reduce(f32[2,64]{1,0:T(2,128)S(1)} %get-tuple-element.47, f32[2,64]{1,0:T(2,128)S(1)} %get-tuple-element.48), channel_id=1, replica_groups=mesh['group'=32,'vocab'=16] {'vocab'}, use_global_device_ids=true, to_apply=%region_2.4 | all-reduce | flops 256 | bytes 2048 | tf_op jit(solution)/shard_map/psum | solution.py:85
  152.0 28.5 %all-gather.9.cloned.1.call-done = bf16[2,128,2048]{1,2,0:T(8,128)(2,1)} async-done(((bf16[2,128,64]{1,2,0:T(8,128)(2,1)}), bf16[2,128,2048]{1,2,0:T(8,128)(2,1)}) %all-gather.9.cloned.1.call-update) | async-done | bytes 1048592 | tf_op jit(solution)/shard_map/all_gather | solution.py:157
  180.5 2.3 copy.117
  182.8 6.5 %all-to-all-start.2 = ((bf16[16,2,128,128]{3,2,1,0:T(8,128)(2,1)}), bf16[16,2,128,128]{3,2,1,0:T(8,128)(2,1)S(1)}, u32[]{:S(2)}, u32[]{:S(2)}) async-start(bf16[16,2,128,128]{3,2,1,0:T(8,128)(2,1)} %copy.117), calls=%async_computation.2 | async-start | bytes 2097152 | tf_op jit(solution)/shard_map/all_to_all | solution.py:161
  190.6 1.4 fusion.8
  192.0 1.1 fusion.11
  193.0 24.7 %all-gather = bf16[2,64,1,2048]{3,1,0,2:T(8,128)(2,1)S(1)} all-gather(bf16[2,64,1,128]{3,1,0,2:T(8,128)(2,1)S(1)} %fusion.11), channel_id=2, replica_groups=mesh['group'=32,'vocab'=16] {'vocab'}, dimensions={3}, use_global_device_ids=true | all-gather | bytes 557056 | tf_op jit(solution)/shard_map/all_gather | solution.py:163
  218.9 56.9 %all-gather.11.cloned.1.call-done = f32[2,64,2048]{2,1,0:T(8,128)} async-done(((f32[2,64,128]{2,1,0:T(8,128)}), f32[2,64,2048]{2,1,0:T(8,128)}) %all-gather.11.cloned.1.call-update) | async-done | bytes 1048592 | tf_op jit(solution)/shard_map/all_gather | solution.py:167
  275.7 1.4 multiply_reduce_fusion
  277.1 1.7 fusion.12
  281.8 106.4 %all-gather.13.cloned.1.call-done = bf16[2,2048,2048]{2,1,0:T(8,128)(2,1)} async-done(((bf16[2,64,2048]{2,1,0:T(8,128)(2,1)}), bf16[2,2048,2048]{2,1,0:T(8,128)(2,1)}) %all-gather.13.cloned.1.call-update) | async-done | bytes 16777232 | tf_op jit(solution)/shard_map/all_gather | solution.py:177
  388.3 11.1 %fusion.68 = (f32[2,2048]{1,0:T(2,128)S(1)}, f32[2,2048,196]{1,2,0:T(8,128)}) fusion(bf16[2,2048,2048]{2,1,0:T(8,128)(2,1)} %all-gather.13.cloned.1.call-done, bf16[2,2048,196]{1,0,2:T(2,128)(2,1)S(1)} %copy-done), kind=kOutput, calls=%fused_computation.172 | convolution fusion | flops 3289133056 | bytes 21610496 | tf_op jit(solution)/shard_map/mtd,mdv->mtv/dot_general | solution.py:175
  399.5 2.8 exponential_reduce_fusion
  404.9 9.1 %all-to-all-start.3 = ((f32[32,1,1152]{2,1,0:T(1,128)}), f32[32,1,1152]{2,1,0:T(1,128)S(1)}, u32[]{:S(2)}, u32[]{:S(2)}) async-start(f32[32,1,1152]{2,1,0:T(1,128)} %reshape.549), calls=%async_computation.3 | async-start | bytes 294912 | tf_op jit(solution)/shard_map/all_to_all | solution.py:205
  415.2 15.2 %all-to-all-done.3 = f32[32,1,1152]{2,1,0:T(1,128)S(1)} async-done(((f32[32,1,1152]{2,1,0:T(1,128)}), f32[32,1,1152]{2,1,0:T(1,128)S(1)}, u32[]{:S(2)}, u32[]{:S(2)}) %all-to-all-start.3) | async-done | bytes 147488 | tf_op jit(solution)/shard_map/all_to_all | solution.py:205
  430.9 1.0 reduce.8
  432.4 18.6 %all-gather.1 = f32[48,3,2,64]{3,2,1,0:T(2,128)S(1)} all-gather(f32[3,3,2,64]{3,2,1,0:T(2,128)S(1)} %pad_maximum_fusion.3), channel_id=3, replica_groups=mesh['group'=32,'vocab'=16] {'vocab'}, dimensions={0}, use_global_device_ids=true | all-gather | bytes 78336 | tf_op jit(solution)/shard_map/all_gather | solution.py:209
  (124 shorter events, 22.9 us)
Async XLA Ops:
  7.2 381.1 %copy-start = (bf16[2,2048,196]{1,0,2:T(2,128)(2,1)S(1)}, bf16[2,2048,196]{1,0,2:T(2,128)(2,1)}, u32[]{:S(2)}) copy-start(bf16[2,2048,196]{1,0,2:T(2,128)(2,1)} %param.27) | copy-start | bytes 4816900
  7.2 106.7 %all-gather.7.cloned.1.call-start = ((), (), s32[]{:S(2)}) async-start(), calls=%async_computation.4 | async-start | bytes 3244032 | tf_op jit(solution)/shard_map/all_gather | solution.py:79
  16.3 59.9 %copy-start.7 = (s32[64]{0:T(128)S(1)}, s32[64]{0:T(128)}, u32[]{:S(2)}) copy-start(s32[64]{0:T(128)} %param.31) | copy-start | bytes 772
  16.3 60.0 %copy-start.6 = (s32[32,64]{1,0:T(8,128)S(1)}, s32[32,64]{1,0:T(8,128)}, u32[]{:S(2)}) copy-start(s32[32,64]{1,0:T(8,128)} %param.33) | copy-start | bytes 24580
  16.3 60.0 %copy-start.8 = (s32[64]{0:T(128)S(1)}, s32[64]{0:T(128)}, u32[]{:S(2)}) copy-start(s32[64]{0:T(128)} %param.32) | copy-start | bytes 772
  17.4 54.6 %all-to-all-start = ((bf16[2,2,1,32,16,128]{5,4,1,0,2,3:T(8,128)(2,1)}), bf16[2,2,1,32,16,128]{5,4,1,0,2,3:T(8,128)(2,1)S(1)}, u32[]{:S(2)}, u32[]{:S(2)}) async-start(bf16[2,2,1,32,16,128]{5,4,1,0,2,3:T(8,128)(2,1)} %copy.110), calls=%async_computation | async-start | bytes 1048576 | tf_op jit(solution)/shard_map/all_to_all | solution.py:117
  72.0 41.9 %all-to-all-start.1 = ((bf16[2,2,1,32,16,128]{5,4,1,0,2,3:T(8,128)(2,1)}), bf16[2,2,1,32,16,128]{5,4,1,0,2,3:T(8,128)(2,1)S(1)}, u32[]{:S(2)}, u32[]{:S(2)}) async-start(bf16[2,2,1,32,16,128]{5,4,1,0,2,3:T(8,128)(2,1)} %copy.112), calls=%async_computation.1 | async-start | bytes 1048576 | tf_op jit(solution)/shard_map/all_to_all | solution.py:116
  76.1 104.4 %all-gather.9.cloned.1.call-start = ((), (), s32[]{:S(2)}) async-start(), calls=%async_computation.5 | async-start | bytes 1081344 | tf_op jit(solution)/shard_map/all_gather | solution.py:157
  77.2 73.1 %copy-start.4 = (f32[2,128]{1,0:T(2,128)S(1)}, f32[2,128]{1,0:T(2,128)}, u32[]{:S(2)}) copy-start(f32[2,128]{1,0:T(2,128)} %param.23) | copy-start | bytes 3076
  77.2 73.2 %copy-start.5 = (f32[2,128]{1,0:T(2,128)S(1)}, f32[2,128]{1,0:T(2,128)}, u32[]{:S(2)}) copy-start(f32[2,128]{1,0:T(2,128)} %param.24) | copy-start | bytes 3076
  182.8 34.9 %all-to-all-start.2 = ((bf16[16,2,128,128]{3,2,1,0:T(8,128)(2,1)}), bf16[16,2,128,128]{3,2,1,0:T(8,128)(2,1)S(1)}, u32[]{:S(2)}, u32[]{:S(2)}) async-start(bf16[16,2,128,128]{3,2,1,0:T(8,128)(2,1)} %copy.117), calls=%async_computation.2 | async-start | bytes 2097152 | tf_op jit(solution)/shard_map/all_to_all | solution.py:161
  189.3 86.4 %all-gather.11.cloned.1.call-start = ((), (), s32[]{:S(2)}) async-start(), calls=%async_computation.6 | async-start | bytes 1114112 | tf_op jit(solution)/shard_map/all_gather | solution.py:167
  190.6 86.5 %copy-start.1 = (f32[2,2048]{1,0:T(2,128)S(1)}, f32[2,2048]{1,0:T(2,128)}, u32[]{:S(2)}) copy-start(f32[2,2048]{1,0:T(2,128)} %param.25) | copy-start | bytes 49156
  217.7 61.1 %copy-start.2 = (f32[2,2048]{1,0:T(2,128)S(1)}, f32[2,2048]{1,0:T(2,128)}, u32[]{:S(2)}) copy-start(f32[2,2048]{1,0:T(2,128)} %param.26) | copy-start | bytes 49156
  218.8 62.8 %copy-start.3 = (s32[2048]{0:T(1024)S(1)}, s32[2048]{0:T(1024)}, u32[]{:S(2)}) copy-start(s32[2048]{0:T(1024)} %param.34) | copy-start | bytes 24580
  218.8 169.5 %all-gather.13.cloned.1.call-start = ((), (), s32[]{:S(2)}) async-start(), calls=%async_computation.7 | async-start | bytes 17301504 | tf_op jit(solution)/shard_map/all_gather | solution.py:177
  404.9 25.6 %all-to-all-start.3 = ((f32[32,1,1152]{2,1,0:T(1,128)}), f32[32,1,1152]{2,1,0:T(1,128)S(1)}, u32[]{:S(2)}, u32[]{:S(2)}) async-start(f32[32,1,1152]{2,1,0:T(1,128)} %reshape.549), calls=%async_computation.3 | async-start | bytes 294912 | tf_op jit(solution)/shard_map/all_to_all | solution.py:205
Sparse Core Ops, SparseCore 0:
  10.1 99.0 all-gather.6
  114.1 66.4 all-gather.8
  218.9 56.7 all-gather.10
  280.0 108.1 all-gather.12

commit v4 on v3

--- a/solution.py
+++ b/solution.py
@@ -76,15 +76,26 @@
     heads_dev = HEADS // vocab_count
     score_scale = 1.0 / math.sqrt(head_size)
     request_count = deal.shape[0]
-    qkv_rows = lax.all_gather(qkv_weight, "group", axis=1, tiled=True)
-    qkv_rows, out_weight = lax.optimization_barrier((qkv_rows, out_weight))
+    qkv_size = qkv_weight.size
+    both_weights = lax.all_gather(
+        jnp.concatenate((qkv_weight.reshape(-1), out_weight.reshape(-1))), "group"
+    )
+    qkv_rows = jnp.transpose(
+        both_weights[:, :qkv_size].reshape((groups,) + qkv_weight.shape), (1, 0, 2, 3)
+    ).reshape(2, groups * qkv_weight.shape[1], qkv_weight.shape[2])
+    head_rows = jnp.transpose(
+        both_weights[:, qkv_size:].reshape((groups,) + out_weight.shape), (1, 2, 0, 3)
+    ).reshape(2, out_weight.shape[1], groups * out_weight.shape[2])
     united = jnp.einsum("mtd,mdc->mtc", hidden_in, qkv_rows, preferred_element_type=jnp.float32)
     united = united.reshape(2, TOK_G, heads_dev, 3, head_size)
     query_raw = united[:, :, :, 0, :].reshape(2, TOK_G, heads_dev * head_size)
     key_raw = united[:, :, :, 1, :].reshape(2, TOK_G, heads_dev * head_size)
-    query_sq, key_sq = lax.psum(
-        (jnp.sum(query_raw * query_raw, axis=-1), jnp.sum(key_raw * key_raw, axis=-1)), "vocab"
-    )
+    squares = lax.all_gather(
+        jnp.stack((jnp.sum(query_raw * query_raw, axis=-1), jnp.sum(key_raw * key_raw, axis=-1))),
+        "vocab",
+    )
+    query_sq = jnp.sum(squares[:, 0], axis=0)
+    key_sq = jnp.sum(squares[:, 1], axis=0)
     query_normed = query_raw * lax.rsqrt(query_sq[..., None] / D + EPS) * q_gain[:, None, :]
     key_normed = key_raw * lax.rsqrt(key_sq[..., None] / D + EPS) * k_gain[:, None, :]
     seg_ids = lax.dynamic_index_in_dim(segment_ids, group_idx, 0, keepdims=False)
@@ -154,7 +165,6 @@
         .astype(jnp.bfloat16)
     )
     col_width = D // vocab_count
-    head_rows = lax.all_gather(out_weight, "group", axis=2, tiled=True)
     head_rows = jnp.transpose(
         head_rows.reshape(2, heads_dev * head_size, vocab_count, col_width), (2, 0, 1, 3)
     )

time: 465 us -> 449 us (0.966)
  waiting for transfers between devices: 281 us -> 257 us
  local copies, waits for them, and re-layouts: 17 us -> 38.9 us
  blocking collectives: 76.7 us -> 58.1 us
    psum x1 -> x0, blocking collectives: 33.4 us -> none  [shards(): lax.psum((jnp.sum(query_raw * query_raw, axis=-1), jnp.sum(key_raw * key_...]
    all_gather x2 -> x1, waiting for transfers between devices: 28.5 us -> 1.47 us  [shards(): lax.all_gather(jnp.concatenate((qkv_weight.reshape(-1), out_weight.reshap...]
    all_gather x0 -> x1, blocking collectives: none -> 21.3 us  [shards(): lax.all_gather(jnp.stack((jnp.sum(query_raw * query_raw, axis=-1), jnp.su...]
    all_gather x1, waiting for transfers between devices: 56.9 us -> 63.6 us  [shards(): mixed = lax.all_gather(mixed_block, 'vocab', axis=2, tiled=True)]
    all_gather x1, blocking collectives: 24.7 us -> 18.2 us  [shards(): attended_all = lax.all_gather(attended, 'vocab', axis=2, tiled=True)]
    all_gather x0 -> x1, local copies, waits for them, and re-layouts: none -> 5.52 us  [shards(): lax.all_gather(jnp.concatenate((qkv_weight.reshape(-1), out_weight.reshap...]
  transfers between devices with their start and end apart: 8 -> 7, of which waited for: 6 -> 6; matrix products, arithmetic and copies ran while one was open for 5% -> 6% of each run, Pallas kernels for 0% -> 0%
where the time goes in v4:
time: 449 us; the launch traced here: 442 us
  waiting for transfers between devices  257 us (57%)
  blocking collectives  58.1 us (13%)
  local copies, waits for them, and re-layouts  38.9 us (9%)
  starting transfers between devices  38 us (8%)
  other arithmetic  18.1 us (4%)
  matrix products  17.5 us (4%)
  between operations  14.3 us (3%)
    all_gather x1, waiting for transfers between devices, shards(): lax.all_gather(final, 'group', axis=1, tiled=True)  106 us
    all_gather x1, waiting for transfers between devices, shards(): mixed = lax.all_gather(mixed_block, 'vocab', axis=2, tiled=True)  63.6 us
    all_to_all x1, waiting for transfers between devices, shards(): lax.all_to_all(send_values, 'group', split_axis=3, concat_axis=3, tiled=T...  35.6 us
    all_to_all x1, waiting for transfers between devices, shards(): lax.all_to_all(send_keys, 'group', split_axis=3, concat_axis=3, tiled=True)  35.2 us
    all_gather x1, blocking collectives, shards(): lax.all_gather(jnp.stack((jnp.sum(query_raw * query_raw, axis=-1), jnp.su...  21.3 us
    all_gather x1, blocking collectives, shards(): lax.all_gather(jnp.stack((peak_one, mass_one, target_one), axis=0), 'vocab')  18.6 us
    all_gather x1, blocking collectives, shards(): attended_all = lax.all_gather(attended, 'vocab', axis=2, tiled=True)  18.2 us
    all_to_all x1, starting transfers between devices, shards(): lax.all_to_all(send_values, 'group', split_axis=3, concat_axis=3, tiled=T...  16.7 us
  transfers between devices with their start and end apart: 7, of which 6 were waited for; matrix products, arithmetic and copies ran while one was open for 6% of the time, Pallas kernels for 0%

profile of v4, /device:TPU:1, one launch (start us, length us, event | category | flops | bytes accessed | tf_op | source)
XLA Modules:
  0.0 442.4 jit_solution(2012865969023516213)
XLA Ops:
  14.8 1.7 gather_fusion.4
  16.6 1.7 gather_fusion.3
  19.4 16.7 %all-to-all-start = ((bf16[2,2,1,32,16,128]{5,4,1,0,2,3:T(8,128)(2,1)}), bf16[2,2,1,32,16,128]{5,4,1,0,2,3:T(8,128)(2,1)S(1)}, u32[]{:S(2)}, u32[]{:S(2)}) async-start(bf16[2,2,1,32,16,128]{5,4,1,0,2,3:T(8,128)(2,1)} %copy.122), calls=%async_computation | async-start | bytes 1048576 | tf_op jit(solution)/shard_map/all_to_all | solution.py:128
  37.0 35.6 %all-to-all-done = bf16[2,2,1,32,16,128]{5,4,1,0,2,3:T(8,128)(2,1)S(1)} async-done(((bf16[2,2,1,32,16,128]{5,4,1,0,2,3:T(8,128)(2,1)}), bf16[2,2,1,32,16,128]{5,4,1,0,2,3:T(8,128)(2,1)S(1)}, u32[]{:S(2)}, u32[]{:S(2)}) %all-to-all-start) | async-done | bytes 524320 | tf_op jit(solution)/shard_map/all_to_all | solution.py:128
  72.6 5.4 %all-to-all-start.1 = ((bf16[2,2,1,32,16,128]{5,4,1,0,2,3:T(8,128)(2,1)}), bf16[2,2,1,32,16,128]{5,4,1,0,2,3:T(8,128)(2,1)S(1)}, u32[]{:S(2)}, u32[]{:S(2)}) async-start(bf16[2,2,1,32,16,128]{5,4,1,0,2,3:T(8,128)(2,1)} %copy.124), calls=%async_computation.1 | async-start | bytes 1048576 | tf_op jit(solution)/shard_map/all_to_all | solution.py:127
  80.4 35.2 %all-to-all-done.1 = bf16[2,2,1,32,16,128]{5,4,1,0,2,3:T(8,128)(2,1)S(1)} async-done(((bf16[2,2,1,32,16,128]{5,4,1,0,2,3:T(8,128)(2,1)}), bf16[2,2,1,32,16,128]{5,4,1,0,2,3:T(8,128)(2,1)S(1)}, u32[]{:S(2)}, u32[]{:S(2)}) %all-to-all-start.1) | async-done | bytes 524320 | tf_op jit(solution)/shard_map/all_to_all | solution.py:127
  116.5 1.5 all-gather.12.cloned.1.call-done
  118.0 5.5 %reshape.547 = bf16[32,65536]{1,0:T(8,128)(2,1)} reshape(bf16[2097152]{0:T(1024)(128)(2,1)} %all-gather.12.cloned.1.call-done) | data formatting | bytes 8388608 | tf_op jit(solution)/shard_map/all_gather | solution.py:80
  123.5 3.8 slice.97
  127.3 3.2 reshape.488
  130.6 2.0 copy.131
  133.7 6.4 %all-to-all-start.2 = ((bf16[16,2,128,128]{2,3,1,0:T(8,128)(2,1)}), bf16[16,2,128,128]{2,3,1,0:T(8,128)(2,1)S(1)}, u32[]{:S(2)}, u32[]{:S(2)}) async-start(bf16[16,2,128,128]{2,3,1,0:T(8,128)(2,1)} %copy.132), calls=%async_computation.2 | async-start | bytes 2097152 | tf_op jit(solution)/shard_map/all_to_all | solution.py:171
  140.1 2.5 copy.152
  146.3 21.3 %all-gather.1 = f32[32,2,64]{2,1,0:T(2,128)S(1)} all-gather(f32[2,2,64]{2,1,0:T(2,128)S(1)} %pad_maximum_fusion.5), channel_id=3, replica_groups=mesh['group'=32,'vocab'=16] {'vocab'}, dimensions={0}, use_global_device_ids=true | all-gather | bytes 17408 | tf_op jit(solution)/shard_map/all_gather | solution.py:93
  173.5 18.2 %all-gather.2 = bf16[2,64,1,2048]{3,1,0,2:T(8,128)(2,1)S(1)} all-gather(bf16[2,64,1,128]{3,1,0,2:T(8,128)(2,1)S(1)} %fusion.11), channel_id=4, replica_groups=mesh['group'=32,'vocab'=16] {'vocab'}, dimensions={3}, use_global_device_ids=true | all-gather | bytes 557056 | tf_op jit(solution)/shard_map/all_gather | solution.py:173
  193.1 2.2 fusion.15
  195.5 63.6 %all-gather.8.cloned.1.call-done = f32[2,64,2048]{2,1,0:T(8,128)} async-done(((f32[2,64,128]{2,1,0:T(8,128)}), f32[2,64,2048]{2,1,0:T(8,128)}) %all-gather.8.cloned.1.call-update) | async-done | bytes 1048592 | tf_op jit(solution)/shard_map/all_gather | solution.py:177
  260.5 1.7 fusion.12
  265.2 106.4 %all-gather.10.cloned.1.call-done = bf16[2,2048,2048]{2,1,0:T(8,128)(2,1)} async-done(((bf16[2,64,2048]{2,1,0:T(8,128)(2,1)}), bf16[2,2048,2048]{2,1,0:T(8,128)(2,1)}) %all-gather.10.cloned.1.call-update) | async-done | bytes 16777232 | tf_op jit(solution)/shard_map/all_gather | solution.py:187
  371.6 11.1 %fusion.68 = (f32[2,2048]{1,0:T(2,128)S(1)}, f32[2,2048,196]{1,2,0:T(8,128)}) fusion(bf16[2,2048,2048]{2,1,0:T(8,128)(2,1)} %all-gather.10.cloned.1.call-done, bf16[2,2048,196]{1,0,2:T(2,128)(2,1)S(1)} %copy-done), kind=kOutput, calls=%fused_computation.176 | convolution fusion | flops 3289133056 | bytes 21610496 | tf_op jit(solution)/shard_map/mtd,mdv->mtv/dot_general | solution.py:185
  382.9 2.8 exponential_reduce_fusion
  388.2 9.1 %all-to-all-start.3 = ((f32[32,1,1152]{2,1,0:T(1,128)}), f32[32,1,1152]{2,1,0:T(1,128)S(1)}, u32[]{:S(2)}, u32[]{:S(2)}) async-start(f32[32,1,1152]{2,1,0:T(1,128)} %reshape.575), calls=%async_computation.3 | async-start | bytes 294912 | tf_op jit(solution)/shard_map/all_to_all | solution.py:215
  398.6 15.2 %all-to-all-done.3 = f32[32,1,1152]{2,1,0:T(1,128)S(1)} async-done(((f32[32,1,1152]{2,1,0:T(1,128)}), f32[32,1,1152]{2,1,0:T(1,128)S(1)}, u32[]{:S(2)}, u32[]{:S(2)}) %all-to-all-start.3) | async-done | bytes 147488 | tf_op jit(solution)/shard_map/all_to_all | solution.py:215
  415.8 18.6 %all-gather.3 = f32[48,3,2,64]{3,2,1,0:T(2,128)S(1)} all-gather(f32[3,3,2,64]{3,2,1,0:T(2,128)S(1)} %pad_maximum_fusion.4), channel_id=5, replica_groups=mesh['group'=32,'vocab'=16] {'vocab'}, dimensions={0}, use_global_device_ids=true | all-gather | bytes 78336 | tf_op jit(solution)/shard_map/all_gather | solution.py:219
  (138 shorter events, 36.4 us)
Async XLA Ops:
  7.2 364.5 %copy-start = (bf16[2,2048,196]{1,0,2:T(2,128)(2,1)S(1)}, bf16[2,2048,196]{1,0,2:T(2,128)(2,1)}, u32[]{:S(2)}) copy-start(bf16[2,2048,196]{1,0,2:T(2,128)(2,1)} %param.27) | copy-start | bytes 4816900
  7.2 110.8 %all-gather.12.cloned.1.call-start = ((), (), s32[]{:S(2)}) async-start(), calls=%async_computation.6 | async-start | bytes 4325376 | tf_op jit(solution)/shard_map/all_gather | solution.py:80
  12.4 0.7 copy-start.6
  18.3 59.7 %copy-start.8 = (s32[64]{0:T(128)S(1)}, s32[64]{0:T(128)}, u32[]{:S(2)}) copy-start(s32[64]{0:T(128)} %param.31) | copy-start | bytes 772
  18.3 60.5 %copy-start.9 = (s32[64]{0:T(128)S(1)}, s32[64]{0:T(128)}, u32[]{:S(2)}) copy-start(s32[64]{0:T(128)} %param.32) | copy-start | bytes 772
  19.4 53.2 %all-to-all-start = ((bf16[2,2,1,32,16,128]{5,4,1,0,2,3:T(8,128)(2,1)}), bf16[2,2,1,32,16,128]{5,4,1,0,2,3:T(8,128)(2,1)S(1)}, u32[]{:S(2)}, u32[]{:S(2)}) async-start(bf16[2,2,1,32,16,128]{5,4,1,0,2,3:T(8,128)(2,1)} %copy.122), calls=%async_computation | async-start | bytes 1048576 | tf_op jit(solution)/shard_map/all_to_all | solution.py:128
  72.6 43.0 %all-to-all-start.1 = ((bf16[2,2,1,32,16,128]{5,4,1,0,2,3:T(8,128)(2,1)}), bf16[2,2,1,32,16,128]{5,4,1,0,2,3:T(8,128)(2,1)S(1)}, u32[]{:S(2)}, u32[]{:S(2)}) async-start(bf16[2,2,1,32,16,128]{5,4,1,0,2,3:T(8,128)(2,1)} %copy.124), calls=%async_computation.1 | async-start | bytes 1048576 | tf_op jit(solution)/shard_map/all_to_all | solution.py:127
  123.5 3.9 slice-start
  133.7 58.1 %all-to-all-start.2 = ((bf16[16,2,128,128]{2,3,1,0:T(8,128)(2,1)}), bf16[16,2,128,128]{2,3,1,0:T(8,128)(2,1)S(1)}, u32[]{:S(2)}, u32[]{:S(2)}) async-start(bf16[16,2,128,128]{2,3,1,0:T(8,128)(2,1)} %copy.132), calls=%async_computation.2 | async-start | bytes 2097152 | tf_op jit(solution)/shard_map/all_to_all | solution.py:171
  140.1 119.0 %all-gather.8.cloned.1.call-start = ((), (), s32[]{:S(2)}) async-start(), calls=%async_computation.4 | async-start | bytes 1114112 | tf_op jit(solution)/shard_map/all_gather | solution.py:177
  142.6 1.0 copy-start.1
  173.0 87.5 %copy-start.2 = (f32[2,2048]{1,0:T(2,128)S(1)}, f32[2,2048]{1,0:T(2,128)}, u32[]{:S(2)}) copy-start(f32[2,2048]{1,0:T(2,128)} %param.25) | copy-start | bytes 49156
  191.7 70.5 %copy-start.3 = (f32[2,2048]{1,0:T(2,128)S(1)}, f32[2,2048]{1,0:T(2,128)}, u32[]{:S(2)}) copy-start(f32[2,2048]{1,0:T(2,128)} %param.26) | copy-start | bytes 49156
  193.1 70.2 %copy-start.7 = (s32[64]{0:T(128)S(1)}, s32[64]{0:T(128)}, u32[]{:S(2)}) copy-start(s32[64]{0:T(128)} %copy-done.6) | copy-start | bytes 772
  195.3 69.6 %copy-start.4 = (s32[2048]{0:T(1024)S(1)}, s32[2048]{0:T(1024)}, u32[]{:S(2)}) copy-start(s32[2048]{0:T(1024)} %param.34) | copy-start | bytes 24580
  195.3 176.3 %all-gather.10.cloned.1.call-start = ((), (), s32[]{:S(2)}) async-start(), calls=%async_computation.5 | async-start | bytes 17301504 | tf_op jit(solution)/shard_map/all_gather | solution.py:187
  382.8 14.6 %copy-start.5 = (s32[32,64]{1,0:T(8,128)S(1)}, s32[32,64]{1,0:T(8,128)}, u32[]{:S(2)}) copy-start(s32[32,64]{1,0:T(8,128)} %param.33) | copy-start | bytes 24580
  388.2 25.6 %all-to-all-start.3 = ((f32[32,1,1152]{2,1,0:T(1,128)}), f32[32,1,1152]{2,1,0:T(1,128)S(1)}, u32[]{:S(2)}, u32[]{:S(2)}) async-start(f32[32,1,1152]{2,1,0:T(1,128)} %reshape.575), calls=%async_computation.3 | async-start | bytes 294912 | tf_op jit(solution)/shard_map/all_to_all | solution.py:215
Sparse Core Ops, SparseCore 0:
  10.1 107.8 all-gather.11
  195.4 63.6 all-gather.7
  263.4 108.1 all-gather.9

commit v5 on v4

--- a/solution.py
+++ b/solution.py
@@ -76,17 +76,24 @@
     heads_dev = HEADS // vocab_count
     score_scale = 1.0 / math.sqrt(head_size)
     request_count = deal.shape[0]
-    qkv_size = qkv_weight.size
+    lane = head_size
+    parts = qkv_weight.shape[2] // lane
+    rows_here = qkv_weight.shape[1]
+    qkv_local = jnp.transpose(qkv_weight.reshape(2, rows_here, parts, lane), (0, 2, 1, 3))
     both_weights = lax.all_gather(
-        jnp.concatenate((qkv_weight.reshape(-1), out_weight.reshape(-1))), "group"
-    )
-    qkv_rows = jnp.transpose(
-        both_weights[:, :qkv_size].reshape((groups,) + qkv_weight.shape), (1, 0, 2, 3)
-    ).reshape(2, groups * qkv_weight.shape[1], qkv_weight.shape[2])
-    head_rows = jnp.transpose(
-        both_weights[:, qkv_size:].reshape((groups,) + out_weight.shape), (1, 2, 0, 3)
-    ).reshape(2, out_weight.shape[1], groups * out_weight.shape[2])
-    united = jnp.einsum("mtd,mdc->mtc", hidden_in, qkv_rows, preferred_element_type=jnp.float32)
+        jnp.concatenate(
+            (qkv_local.reshape(2, parts * rows_here, lane), out_weight.reshape(2, -1, lane)), axis=1
+        ),
+        "group",
+    )
+    qkv_rows = both_weights[:, :, : parts * rows_here].reshape(groups, 2, parts, rows_here, lane)
+    out_rows = both_weights[:, :, parts * rows_here :].reshape((groups,) + out_weight.shape)
+    united = jnp.einsum(
+        "mtgr,gmjrl->mtjl",
+        hidden_in.reshape(2, TOK_G, groups, rows_here),
+        qkv_rows,
+        preferred_element_type=jnp.float32,
+    )
     united = united.reshape(2, TOK_G, heads_dev, 3, head_size)
     query_raw = united[:, :, :, 0, :].reshape(2, TOK_G, heads_dev * head_size)
     key_raw = united[:, :, :, 1, :].reshape(2, TOK_G, heads_dev * head_size)
@@ -165,9 +172,10 @@
         .astype(jnp.bfloat16)
     )
     col_width = D // vocab_count
+    pair = groups // vocab_count
     head_rows = jnp.transpose(
-        head_rows.reshape(2, heads_dev * head_size, vocab_count, col_width), (2, 0, 1, 3)
-    )
+        out_rows.reshape((vocab_count, pair) + out_weight.shape), (0, 2, 3, 1, 4)
+    ).reshape(vocab_count, 2, heads_dev * head_size, col_width)
     column_block = lax.all_to_all(head_rows, "vocab", split_axis=0, concat_axis=0, tiled=True)
     column_block = jnp.transpose(column_block, (1, 0, 2, 3)).reshape(2, D, col_width)
     attended_all = lax.all_gather(attended, "vocab", axis=2, tiled=True)

time: 449 us -> 440 us (0.980)
  local copies, waits for them, and re-layouts: 38.9 us -> 31.6 us
    all_gather x1 -> x0, local copies, waits for them, and re-layouts: 5.52 us -> none  [shards(): lax.all_gather(jnp.concatenate((qkv_weight.reshape(-1), out_weight.reshap...]
where the time goes in v5:
time: 440 us; the launch traced here: 433 us
  waiting for transfers between devices  255 us (58%)
  blocking collectives  61.2 us (14%)
  starting transfers between devices  37.7 us (9%)
  local copies, waits for them, and re-layouts  31.6 us (7%)
  matrix products  17.8 us (4%)
  other arithmetic  15.8 us (4%)
  between operations  14.3 us (3%)
    all_gather x1, waiting for transfers between devices, shards(): lax.all_gather(final, 'group', axis=1, tiled=True)  106 us
    all_gather x1, waiting for transfers between devices, shards(): mixed = lax.all_gather(mixed_block, 'vocab', axis=2, tiled=True)  63.2 us
    all_to_all x1, waiting for transfers between devices, shards(): lax.all_to_all(send_values, 'group', split_axis=3, concat_axis=3, tiled=T...  35.7 us
    all_to_all x1, waiting for transfers between devices, shards(): lax.all_to_all(send_keys, 'group', split_axis=3, concat_axis=3, tiled=True)  34.1 us
    all_gather x1, blocking collectives, shards(): lax.all_gather(jnp.stack((jnp.sum(query_raw * query_raw, axis=-1), jnp.su...  23.7 us
    all_gather x1, blocking collectives, shards(): attended_all = lax.all_gather(attended, 'vocab', axis=2, tiled=True)  18.9 us
    all_gather x1, blocking collectives, shards(): lax.all_gather(jnp.stack((peak_one, mass_one, target_one), axis=0), 'vocab')  18.6 us
    all_to_all x1, starting transfers between devices, shards(): lax.all_to_all(send_values, 'group', split_axis=3, concat_axis=3, tiled=T...  16.7 us
  transfers between devices with their start and end apart: 7, of which 6 were waited for; matrix products, arithmetic and copies ran while one was open for 6% of the time, Pallas kernels for 0%

profile of v5, /device:TPU:1, one launch (start us, length us, event | category | flops | bytes accessed | tf_op | source)
XLA Modules:
  0.0 433.5 jit_solution(11936283644078445860)
XLA Ops:
  14.8 1.7 gather_fusion.4
  16.6 1.7 gather_fusion.3
  20.2 16.7 %all-to-all-start = ((bf16[2,2,1,32,16,128]{5,4,1,0,2,3:T(8,128)(2,1)}), bf16[2,2,1,32,16,128]{5,4,1,0,2,3:T(8,128)(2,1)S(1)}, u32[]{:S(2)}, u32[]{:S(2)}) async-start(bf16[2,2,1,32,16,128]{5,4,1,0,2,3:T(8,128)(2,1)} %copy.120), calls=%async_computation | async-start | bytes 1048576 | tf_op jit(solution)/shard_map/all_to_all | solution.py:135
  37.0 1.9 copy.122
  38.9 35.7 %all-to-all-done = bf16[2,2,1,32,16,128]{5,4,1,0,2,3:T(8,128)(2,1)S(1)} async-done(((bf16[2,2,1,32,16,128]{5,4,1,0,2,3:T(8,128)(2,1)}), bf16[2,2,1,32,16,128]{5,4,1,0,2,3:T(8,128)(2,1)S(1)}, u32[]{:S(2)}, u32[]{:S(2)}) %all-to-all-start) | async-done | bytes 524320 | tf_op jit(solution)/shard_map/all_to_all | solution.py:135
  74.6 4.5 %all-to-all-start.1 = ((bf16[2,2,1,32,16,128]{5,4,1,0,2,3:T(8,128)(2,1)}), bf16[2,2,1,32,16,128]{5,4,1,0,2,3:T(8,128)(2,1)S(1)}, u32[]{:S(2)}, u32[]{:S(2)}) async-start(bf16[2,2,1,32,16,128]{5,4,1,0,2,3:T(8,128)(2,1)} %copy.122), calls=%async_computation.1 | async-start | bytes 1048576 | tf_op jit(solution)/shard_map/all_to_all | solution.py:134
  79.1 2.0 reshape.488
  83.1 34.1 %all-to-all-done.1 = bf16[2,2,1,32,16,128]{5,4,1,0,2,3:T(8,128)(2,1)S(1)} async-done(((bf16[2,2,1,32,16,128]{5,4,1,0,2,3:T(8,128)(2,1)}), bf16[2,2,1,32,16,128]{5,4,1,0,2,3:T(8,128)(2,1)S(1)}, u32[]{:S(2)}, u32[]{:S(2)}) %all-to-all-start.1) | async-done | bytes 524320 | tf_op jit(solution)/shard_map/all_to_all | solution.py:134
  119.7 3.9 slice.97
  123.7 1.9 reshape_reshape.3
  125.5 2.7 copy.129
  128.2 7.0 %all-to-all-start.2 = ((bf16[16,2,128,128]{2,3,1,0:T(8,128)(2,1)}), bf16[16,2,128,128]{2,3,1,0:T(8,128)(2,1)S(1)}, u32[]{:S(2)}, u32[]{:S(2)}) async-start(bf16[16,2,128,128]{2,3,1,0:T(8,128)(2,1)} %bitcast.52), calls=%async_computation.2 | async-start | bytes 2097152 | tf_op jit(solution)/shard_map/all_to_all | solution.py:179
  135.3 3.2 fusion
  138.7 23.7 %all-gather.1 = f32[32,2,64]{2,1,0:T(2,128)S(1)} all-gather(f32[2,2,64]{2,1,0:T(2,128)S(1)} %pad_maximum_fusion.5), channel_id=3, replica_groups=mesh['group'=32,'vocab'=16] {'vocab'}, dimensions={0}, use_global_device_ids=true | all-gather | bytes 17408 | tf_op jit(solution)/shard_map/all_gather | solution.py:100
  164.4 18.9 %all-gather.2 = bf16[2,64,1,2048]{3,1,0,2:T(8,128)(2,1)} all-gather(bf16[2,64,1,128]{3,1,0,2:T(8,128)(2,1)S(1)} %fusion.13), channel_id=4, replica_groups=mesh['group'=32,'vocab'=16] {'vocab'}, dimensions={3}, use_global_device_ids=true | all-gather | bytes 557056 | tf_op jit(solution)/shard_map/all_gather | solution.py:181
  184.6 2.3 fusion.18
  187.1 63.2 %all-gather.8.cloned.1.call-done = f32[2,64,2048]{2,1,0:T(8,128)} async-done(((f32[2,64,128]{2,1,0:T(8,128)}), f32[2,64,2048]{2,1,0:T(8,128)}) %all-gather.8.cloned.1.call-update) | async-done | bytes 1048592 | tf_op jit(solution)/shard_map/all_gather | solution.py:185
  251.7 1.6 fusion.14
  256.3 106.4 %all-gather.10.cloned.1.call-done = bf16[2,2048,2048]{2,1,0:T(8,128)(2,1)} async-done(((bf16[2,64,2048]{2,1,0:T(8,128)(2,1)}), bf16[2,2048,2048]{2,1,0:T(8,128)(2,1)}) %all-gather.10.cloned.1.call-update) | async-done | bytes 16777232 | tf_op jit(solution)/shard_map/all_gather | solution.py:195
  362.8 11.1 %fusion.74 = (f32[2,2048]{1,0:T(2,128)S(1)}, f32[2,2048,196]{1,2,0:T(8,128)}) fusion(bf16[2,2048,2048]{2,1,0:T(8,128)(2,1)} %all-gather.10.cloned.1.call-done, bf16[2,2048,196]{1,0,2:T(2,128)(2,1)S(1)} %copy-done), kind=kOutput, calls=%fused_computation.183 | convolution fusion | flops 3289133056 | bytes 21610496 | tf_op jit(solution)/shard_map/mtd,mdv->mtv/dot_general | solution.py:193
  374.0 2.8 exponential_reduce_fusion
  379.3 9.1 %all-to-all-start.3 = ((f32[32,1,1152]{2,1,0:T(1,128)}), f32[32,1,1152]{2,1,0:T(1,128)S(1)}, u32[]{:S(2)}, u32[]{:S(2)}) async-start(f32[32,1,1152]{2,1,0:T(1,128)} %reshape.581), calls=%async_computation.3 | async-start | bytes 294912 | tf_op jit(solution)/shard_map/all_to_all | solution.py:223
  389.7 15.2 %all-to-all-done.3 = f32[32,1,1152]{2,1,0:T(1,128)S(1)} async-done(((f32[32,1,1152]{2,1,0:T(1,128)}), f32[32,1,1152]{2,1,0:T(1,128)S(1)}, u32[]{:S(2)}, u32[]{:S(2)}) %all-to-all-start.3) | async-done | bytes 147488 | tf_op jit(solution)/shard_map/all_to_all | solution.py:223
  406.9 18.6 %all-gather.3 = f32[48,3,2,64]{3,2,1,0:T(2,128)S(1)} all-gather(f32[3,3,2,64]{3,2,1,0:T(2,128)S(1)} %pad_maximum_fusion.4), channel_id=5, replica_groups=mesh['group'=32,'vocab'=16] {'vocab'}, dimensions={0}, use_global_device_ids=true | all-gather | bytes 78336 | tf_op jit(solution)/shard_map/all_gather | solution.py:227
  (134 shorter events, 29.0 us)
Async XLA Ops:
  7.2 355.6 %copy-start = (bf16[2,2048,196]{1,0,2:T(2,128)(2,1)S(1)}, bf16[2,2048,196]{1,0,2:T(2,128)(2,1)}, u32[]{:S(2)}) copy-start(bf16[2,2048,196]{1,0,2:T(2,128)(2,1)} %param.27) | copy-start | bytes 4816900
  7.2 111.3 %all-gather.12.cloned.1.call-start = ((), (), s32[]{:S(2)}) async-start(), calls=%async_computation.6 | async-start | bytes 4325376 | tf_op jit(solution)/shard_map/all_gather | solution.py:83
  18.3 60.8 %copy-start.1 = (bf16[2,64,2048]{2,1,0:T(8,128)(2,1)S(1)}, bf16[2,64,2048]{2,1,0:T(8,128)(2,1)}, u32[]{:S(2)}) copy-start(bf16[2,64,2048]{2,1,0:T(8,128)(2,1)} %param.20) | copy-start | bytes 1572868
  19.3 61.9 %copy-start.10 = (s32[64]{0:T(128)S(1)}, s32[64]{0:T(128)}, u32[]{:S(2)}) copy-start(s32[64]{0:T(128)} %param.31) | copy-start | bytes 772
  19.3 61.9 %copy-start.9 = (s32[32,64]{1,0:T(8,128)S(1)}, s32[32,64]{1,0:T(8,128)}, u32[]{:S(2)}) copy-start(s32[32,64]{1,0:T(8,128)} %param.33) | copy-start | bytes 24580
  19.3 62.0 %copy-start.11 = (s32[64]{0:T(128)S(1)}, s32[64]{0:T(128)}, u32[]{:S(2)}) copy-start(s32[64]{0:T(128)} %param.32) | copy-start | bytes 772
  20.2 54.4 %all-to-all-start = ((bf16[2,2,1,32,16,128]{5,4,1,0,2,3:T(8,128)(2,1)}), bf16[2,2,1,32,16,128]{5,4,1,0,2,3:T(8,128)(2,1)S(1)}, u32[]{:S(2)}, u32[]{:S(2)}) async-start(bf16[2,2,1,32,16,128]{5,4,1,0,2,3:T(8,128)(2,1)} %copy.120), calls=%async_computation | async-start | bytes 1048576 | tf_op jit(solution)/shard_map/all_to_all | solution.py:135
  74.6 42.6 %all-to-all-start.1 = ((bf16[2,2,1,32,16,128]{5,4,1,0,2,3:T(8,128)(2,1)}), bf16[2,2,1,32,16,128]{5,4,1,0,2,3:T(8,128)(2,1)S(1)}, u32[]{:S(2)}, u32[]{:S(2)}) async-start(bf16[2,2,1,32,16,128]{5,4,1,0,2,3:T(8,128)(2,1)} %copy.122), calls=%async_computation.1 | async-start | bytes 1048576 | tf_op jit(solution)/shard_map/all_to_all | solution.py:134
  128.2 55.0 %all-to-all-start.2 = ((bf16[16,2,128,128]{2,3,1,0:T(8,128)(2,1)}), bf16[16,2,128,128]{2,3,1,0:T(8,128)(2,1)S(1)}, u32[]{:S(2)}, u32[]{:S(2)}) async-start(bf16[16,2,128,128]{2,3,1,0:T(8,128)(2,1)} %bitcast.52), calls=%async_computation.2 | async-start | bytes 2097152 | tf_op jit(solution)/shard_map/all_to_all | solution.py:179
  135.2 27.3 %copy-start.7 = (f32[2,128]{1,0:T(2,128)S(1)}, f32[2,128]{1,0:T(2,128)}, u32[]{:S(2)}) copy-start(f32[2,128]{1,0:T(2,128)} %param.23) | copy-start | bytes 3076
  135.2 27.3 %copy-start.8 = (f32[2,128]{1,0:T(2,128)S(1)}, f32[2,128]{1,0:T(2,128)}, u32[]{:S(2)}) copy-start(f32[2,128]{1,0:T(2,128)} %param.24) | copy-start | bytes 3076
  135.3 115.1 %all-gather.8.cloned.1.call-start = ((), (), s32[]{:S(2)}) async-start(), calls=%async_computation.4 | async-start | bytes 1114112 | tf_op jit(solution)/shard_map/all_gather | solution.py:185
  135.3 27.6 %copy-start.3 = (bf16[2,2,1,32,16,128]{5,4,3,1,0,2:T(8,128)(2,1)S(1)}, bf16[2,2,1,32,16,128]{5,4,3,1,0,2:T(8,128)(2,1)}, u32[]{:S(2)}) copy-start(bf16[2,2,1,32,16,128]{5,4,3,1,0,2:T(8,128)(2,1)} %copy.123) | copy-start | bytes 1572868
  138.6 25.3 %copy-start.2 = (bf16[2,2,1,32,16,128]{5,4,3,1,0,2:T(8,128)(2,1)S(1)}, bf16[2,2,1,32,16,128]{5,4,3,1,0,2:T(8,128)(2,1)}, u32[]{:S(2)}) copy-start(bf16[2,2,1,32,16,128]{5,4,3,1,0,2:T(8,128)(2,1)} %copy.121) | copy-start | bytes 1572868
  163.8 87.9 %copy-start.4 = (f32[2,2048]{1,0:T(2,128)S(1)}, f32[2,2048]{1,0:T(2,128)}, u32[]{:S(2)}) copy-start(f32[2,2048]{1,0:T(2,128)} %param.25) | copy-start | bytes 49156
  183.2 70.2 %copy-start.5 = (f32[2,2048]{1,0:T(2,128)S(1)}, f32[2,2048]{1,0:T(2,128)}, u32[]{:S(2)}) copy-start(f32[2,2048]{1,0:T(2,128)} %param.26) | copy-start | bytes 49156
  186.9 69.2 %copy-start.6 = (s32[2048]{0:T(1024)S(1)}, s32[2048]{0:T(1024)}, u32[]{:S(2)}) copy-start(s32[2048]{0:T(1024)} %param.34) | copy-start | bytes 24580
  186.9 175.8 %all-gather.10.cloned.1.call-start = ((), (), s32[]{:S(2)}) async-start(), calls=%async_computation.5 | async-start | bytes 17301504 | tf_op jit(solution)/shard_map/all_gather | solution.py:195
  379.3 25.6 %all-to-all-start.3 = ((f32[32,1,1152]{2,1,0:T(1,128)}), f32[32,1,1152]{2,1,0:T(1,128)S(1)}, u32[]{:S(2)}, u32[]{:S(2)}) async-start(f32[32,1,1152]{2,1,0:T(1,128)} %reshape.581), calls=%async_computation.3 | async-start | bytes 294912 | tf_op jit(solution)/shard_map/all_to_all | solution.py:223
Sparse Core Ops, SparseCore 0:
  10.1 108.2 all-gather.11
  187.0 63.2 all-gather.7
  254.5 108.1 all-gather.9

commit v6 on v5

--- a/solution.py
+++ b/solution.py
@@ -182,7 +182,9 @@
     mixed_block = jnp.einsum(
         "mtc,mcd->mtd", attended_all, column_block, preferred_element_type=jnp.float32
     )
-    mixed = lax.all_gather(mixed_block, "vocab", axis=2, tiled=True)
+    mixed = lax.all_gather(mixed_block.astype(jnp.bfloat16), "vocab", axis=2, tiled=True).astype(
+        jnp.float32
+    )
     hidden_new = (hidden_in.astype(jnp.float32) + rms_scale(mixed, post_gain[:, None, :])).astype(
         jnp.bfloat16
     )

time: 440 us -> 402 us (0.914)
  waiting for transfers between devices: 255 us -> 202 us
  blocking collectives: 61.2 us -> 80 us
    all_gather x1 -> x0, waiting for transfers between devices: 63.2 us -> none  [shards(): mixed = lax.all_gather(mixed_block, 'vocab', axis=2, tiled=True)]
    all_gather x0 -> x1, blocking collectives: none -> 18.8 us  [shards(): lax.all_gather(mixed_block.astype(jnp.bfloat16), 'vocab', axis=2, tiled=T...]
    all_gather x1, waiting for transfers between devices: 106 us -> 116 us  [shards(): lax.all_gather(final, 'group', axis=1, tiled=True)]
  transfers between devices with their start and end apart: 7 -> 6, of which waited for: 6 -> 4; matrix products, arithmetic and copies ran while one was open for 6% -> 6% of each run, Pallas kernels for 0% -> 0%
where the time goes in v6:
time: 402 us; the launch traced here: 396 us
  waiting for transfers between devices  202 us (50%)
  blocking collectives  80 us (20%)
  starting transfers between devices  37.4 us (9%)
  local copies, waits for them, and re-layouts  31.6 us (8%)
  matrix products  17.2 us (4%)
  between operations  14.6 us (4%)
  other arithmetic  13.5 us (3%)
    all_gather x1, waiting for transfers between devices, shards(): lax.all_gather(final, 'group', axis=1, tiled=True)  116 us
    all_to_all x1, waiting for transfers between devices, shards(): lax.all_to_all(send_values, 'group', split_axis=3, concat_axis=3, tiled=T...  35.8 us
    all_to_all x1, waiting for transfers between devices, shards(): lax.all_to_all(send_keys, 'group', split_axis=3, concat_axis=3, tiled=True)  34.4 us
    all_gather x1, blocking collectives, shards(): lax.all_gather(jnp.stack((jnp.sum(query_raw * query_raw, axis=-1), jnp.su...  23.8 us
    all_gather x1, blocking collectives, shards(): attended_all = lax.all_gather(attended, 'vocab', axis=2, tiled=True)  18.9 us
    all_gather x1, blocking collectives, shards(): lax.all_gather(mixed_block.astype(jnp.bfloat16), 'vocab', axis=2, tiled=T...  18.8 us
    all_gather x1, blocking collectives, shards(): lax.all_gather(jnp.stack((peak_one, mass_one, target_one), axis=0), 'vocab')  18.6 us
    all_to_all x1, starting transfers between devices, shards(): lax.all_to_all(send_values, 'group', split_axis=3, concat_axis=3, tiled=T...  16.7 us
  transfers between devices with their start and end apart: 6, of which 4 were waited for; matrix products, arithmetic and copies ran while one was open for 6% of the time, Pallas kernels for 0%

profile of v6, /device:TPU:1, one launch (start us, length us, event | category | flops | bytes accessed | tf_op | source)
XLA Modules:
  0.0 396.0 jit_solution(9022007774549673888)
XLA Ops:
  14.8 1.7 gather_fusion.4
  16.6 1.7 gather_fusion.3
  20.2 16.7 %all-to-all-start = ((bf16[2,2,1,32,16,128]{5,4,1,0,2,3:T(8,128)(2,1)}), bf16[2,2,1,32,16,128]{5,4,1,0,2,3:T(8,128)(2,1)S(1)}, u32[]{:S(2)}, u32[]{:S(2)}) async-start(bf16[2,2,1,32,16,128]{5,4,1,0,2,3:T(8,128)(2,1)} %copy.120), calls=%async_computation | async-start | bytes 1048576 | tf_op jit(solution)/shard_map/all_to_all | solution.py:135
  37.0 1.9 copy.122
  38.9 35.8 %all-to-all-done = bf16[2,2,1,32,16,128]{5,4,1,0,2,3:T(8,128)(2,1)S(1)} async-done(((bf16[2,2,1,32,16,128]{5,4,1,0,2,3:T(8,128)(2,1)}), bf16[2,2,1,32,16,128]{5,4,1,0,2,3:T(8,128)(2,1)S(1)}, u32[]{:S(2)}, u32[]{:S(2)}) %all-to-all-start) | async-done | bytes 524320 | tf_op jit(solution)/shard_map/all_to_all | solution.py:135
  74.6 4.5 %all-to-all-start.1 = ((bf16[2,2,1,32,16,128]{5,4,1,0,2,3:T(8,128)(2,1)}), bf16[2,2,1,32,16,128]{5,4,1,0,2,3:T(8,128)(2,1)S(1)}, u32[]{:S(2)}, u32[]{:S(2)}) async-start(bf16[2,2,1,32,16,128]{5,4,1,0,2,3:T(8,128)(2,1)} %copy.122), calls=%async_computation.1 | async-start | bytes 1048576 | tf_op jit(solution)/shard_map/all_to_all | solution.py:134
  79.2 2.0 reshape.488
  83.2 34.4 %all-to-all-done.1 = bf16[2,2,1,32,16,128]{5,4,1,0,2,3:T(8,128)(2,1)S(1)} async-done(((bf16[2,2,1,32,16,128]{5,4,1,0,2,3:T(8,128)(2,1)}), bf16[2,2,1,32,16,128]{5,4,1,0,2,3:T(8,128)(2,1)S(1)}, u32[]{:S(2)}, u32[]{:S(2)}) %all-to-all-start.1) | async-done | bytes 524320 | tf_op jit(solution)/shard_map/all_to_all | solution.py:134
  119.8 3.9 slice.97
  123.7 1.9 reshape_reshape.3
  125.6 2.7 copy.129
  128.3 6.9 %all-to-all-start.2 = ((bf16[16,2,128,128]{2,3,1,0:T(8,128)(2,1)}), bf16[16,2,128,128]{2,3,1,0:T(8,128)(2,1)S(1)}, u32[]{:S(2)}, u32[]{:S(2)}) async-start(bf16[16,2,128,128]{2,3,1,0:T(8,128)(2,1)} %bitcast.52), calls=%async_computation.2 | async-start | bytes 2097152 | tf_op jit(solution)/shard_map/all_to_all | solution.py:179
  135.3 3.2 fusion
  138.7 23.8 %all-gather.1 = f32[32,2,64]{2,1,0:T(2,128)S(1)} all-gather(f32[2,2,64]{2,1,0:T(2,128)S(1)} %pad_maximum_fusion.5), channel_id=3, replica_groups=mesh['group'=32,'vocab'=16] {'vocab'}, dimensions={0}, use_global_device_ids=true | all-gather | bytes 17408 | tf_op jit(solution)/shard_map/all_gather | solution.py:100
  164.3 18.9 %all-gather.2 = bf16[2,64,1,2048]{3,1,0,2:T(8,128)(2,1)} all-gather(bf16[2,64,1,128]{3,1,0,2:T(8,128)(2,1)S(1)} %fusion.13), channel_id=4, replica_groups=mesh['group'=32,'vocab'=16] {'vocab'}, dimensions={3}, use_global_device_ids=true | all-gather | bytes 557056 | tf_op jit(solution)/shard_map/all_gather | solution.py:181
  183.2 1.3 copy.130
  184.5 1.7 convolution_convert_fusion
  186.3 18.8 %all_gather.32 = bf16[2,64,2048]{2,1,0:T(8,128)(2,1)S(1)} all-gather(bf16[2,64,128]{2,1,0:T(8,128)(2,1)S(1)} %convolution_convert_fusion), channel_id=1, replica_groups=mesh['group'=32,'vocab'=16] {'vocab'}, dimensions={2}, use_global_device_ids=true | all-gather | bytes 557056 | tf_op jit(solution)/shard_map/all_gather | solution.py:185
  208.7 116.2 %all-gather.7.cloned.1.call-done = bf16[2,2048,2048]{2,1,0:T(8,128)(2,1)} async-done(((bf16[2,64,2048]{2,1,0:T(8,128)(2,1)}), bf16[2,2048,2048]{2,1,0:T(8,128)(2,1)}) %all-gather.7.cloned.1.call-update) | async-done | bytes 16777232 | tf_op jit(solution)/shard_map/all_gather | solution.py:197
  324.9 11.1 %fusion.78 = (f32[2,2048]{1,0:T(2,128)S(1)}, f32[2,2048,196]{1,2,0:T(8,128)}) fusion(bf16[2,2048,2048]{2,1,0:T(8,128)(2,1)} %all-gather.7.cloned.1.call-done, bf16[2,2048,196]{1,0,2:T(2,128)(2,1)S(1)} %copy-done), kind=kOutput, calls=%fused_computation.187 | convolution fusion | flops 3289133056 | bytes 21610496 | tf_op jit(solution)/shard_map/mtd,mdv->mtv/dot_general | solution.py:195
  336.1 2.8 exponential_reduce_fusion
  341.5 9.1 %all-to-all-start.3 = ((f32[32,1,1152]{2,1,0:T(1,128)}), f32[32,1,1152]{2,1,0:T(1,128)S(1)}, u32[]{:S(2)}, u32[]{:S(2)}) async-start(f32[32,1,1152]{2,1,0:T(1,128)} %reshape.581), calls=%async_computation.3 | async-start | bytes 294912 | tf_op jit(solution)/shard_map/all_to_all | solution.py:225
  351.9 15.2 %all-to-all-done.3 = f32[32,1,1152]{2,1,0:T(1,128)S(1)} async-done(((f32[32,1,1152]{2,1,0:T(1,128)}), f32[32,1,1152]{2,1,0:T(1,128)S(1)}, u32[]{:S(2)}, u32[]{:S(2)}) %all-to-all-start.3) | async-done | bytes 147488 | tf_op jit(solution)/shard_map/all_to_all | solution.py:225
  369.1 18.6 %all-gather.3 = f32[48,3,2,64]{3,2,1,0:T(2,128)S(1)} all-gather(f32[3,3,2,64]{3,2,1,0:T(2,128)S(1)} %pad_maximum_fusion.4), channel_id=5, replica_groups=mesh['group'=32,'vocab'=16] {'vocab'}, dimensions={0}, use_global_device_ids=true | all-gather | bytes 78336 | tf_op jit(solution)/shard_map/all_gather | solution.py:229
  (132 shorter events, 26.3 us)
Async XLA Ops:
  7.2 317.7 %copy-start = (bf16[2,2048,196]{1,0,2:T(2,128)(2,1)S(1)}, bf16[2,2048,196]{1,0,2:T(2,128)(2,1)}, u32[]{:S(2)}) copy-start(bf16[2,2048,196]{1,0,2:T(2,128)(2,1)} %param.27) | copy-start | bytes 4816900
  7.2 111.3 %all-gather.9.cloned.1.call-start = ((), (), s32[]{:S(2)}) async-start(), calls=%async_computation.5 | async-start | bytes 4325376 | tf_op jit(solution)/shard_map/all_gather | solution.py:83
  18.3 60.8 %copy-start.1 = (bf16[2,64,2048]{2,1,0:T(8,128)(2,1)S(1)}, bf16[2,64,2048]{2,1,0:T(8,128)(2,1)}, u32[]{:S(2)}) copy-start(bf16[2,64,2048]{2,1,0:T(8,128)(2,1)} %param.20) | copy-start | bytes 1572868
  19.3 61.9 %copy-start.10 = (s32[64]{0:T(128)S(1)}, s32[64]{0:T(128)}, u32[]{:S(2)}) copy-start(s32[64]{0:T(128)} %param.31) | copy-start | bytes 772
  19.3 62.0 %copy-start.9 = (s32[32,64]{1,0:T(8,128)S(1)}, s32[32,64]{1,0:T(8,128)}, u32[]{:S(2)}) copy-start(s32[32,64]{1,0:T(8,128)} %param.33) | copy-start | bytes 24580
  19.3 62.0 %copy-start.11 = (s32[64]{0:T(128)S(1)}, s32[64]{0:T(128)}, u32[]{:S(2)}) copy-start(s32[64]{0:T(128)} %param.32) | copy-start | bytes 772
  20.2 54.4 %all-to-all-start = ((bf16[2,2,1,32,16,128]{5,4,1,0,2,3:T(8,128)(2,1)}), bf16[2,2,1,32,16,128]{5,4,1,0,2,3:T(8,128)(2,1)S(1)}, u32[]{:S(2)}, u32[]{:S(2)}) async-start(bf16[2,2,1,32,16,128]{5,4,1,0,2,3:T(8,128)(2,1)} %copy.120), calls=%async_computation | async-start | bytes 1048576 | tf_op jit(solution)/shard_map/all_to_all | solution.py:135
  74.6 42.9 %all-to-all-start.1 = ((bf16[2,2,1,32,16,128]{5,4,1,0,2,3:T(8,128)(2,1)}), bf16[2,2,1,32,16,128]{5,4,1,0,2,3:T(8,128)(2,1)S(1)}, u32[]{:S(2)}, u32[]{:S(2)}) async-start(bf16[2,2,1,32,16,128]{5,4,1,0,2,3:T(8,128)(2,1)} %copy.122), calls=%async_computation.1 | async-start | bytes 1048576 | tf_op jit(solution)/shard_map/all_to_all | solution.py:134
  128.3 54.9 %all-to-all-start.2 = ((bf16[16,2,128,128]{2,3,1,0:T(8,128)(2,1)}), bf16[16,2,128,128]{2,3,1,0:T(8,128)(2,1)S(1)}, u32[]{:S(2)}, u32[]{:S(2)}) async-start(bf16[16,2,128,128]{2,3,1,0:T(8,128)(2,1)} %bitcast.52), calls=%async_computation.2 | async-start | bytes 2097152 | tf_op jit(solution)/shard_map/all_to_all | solution.py:179
  135.2 27.3 %copy-start.7 = (f32[2,128]{1,0:T(2,128)S(1)}, f32[2,128]{1,0:T(2,128)}, u32[]{:S(2)}) copy-start(f32[2,128]{1,0:T(2,128)} %param.23) | copy-start | bytes 3076
  135.2 27.3 %copy-start.8 = (f32[2,128]{1,0:T(2,128)S(1)}, f32[2,128]{1,0:T(2,128)}, u32[]{:S(2)}) copy-start(f32[2,128]{1,0:T(2,128)} %param.24) | copy-start | bytes 3076
  135.2 189.7 %all-gather.7.cloned.1.call-start = ((), (), s32[]{:S(2)}) async-start(), calls=%async_computation.4 | async-start | bytes 17301504 | tf_op jit(solution)/shard_map/all_gather | solution.py:197
  135.3 27.6 %copy-start.3 = (bf16[2,2,1,32,16,128]{5,4,3,1,0,2:T(8,128)(2,1)S(1)}, bf16[2,2,1,32,16,128]{5,4,3,1,0,2:T(8,128)(2,1)}, u32[]{:S(2)}) copy-start(bf16[2,2,1,32,16,128]{5,4,3,1,0,2:T(8,128)(2,1)} %copy.123) | copy-start | bytes 1572868
  138.5 25.3 %copy-start.2 = (bf16[2,2,1,32,16,128]{5,4,3,1,0,2:T(8,128)(2,1)S(1)}, bf16[2,2,1,32,16,128]{5,4,3,1,0,2:T(8,128)(2,1)}, u32[]{:S(2)}) copy-start(bf16[2,2,1,32,16,128]{5,4,3,1,0,2:T(8,128)(2,1)} %copy.121) | copy-start | bytes 1572868
  163.8 41.5 %copy-start.4 = (f32[2,2048]{1,0:T(2,128)S(1)}, f32[2,2048]{1,0:T(2,128)}, u32[]{:S(2)}) copy-start(f32[2,2048]{1,0:T(2,128)} %param.25) | copy-start | bytes 49156
  183.2 22.5 %copy-start.5 = (f32[2,2048]{1,0:T(2,128)S(1)}, f32[2,2048]{1,0:T(2,128)}, u32[]{:S(2)}) copy-start(f32[2,2048]{1,0:T(2,128)} %param.26) | copy-start | bytes 49156
  184.5 23.9 %copy-start.6 = (s32[2048]{0:T(1024)S(1)}, s32[2048]{0:T(1024)}, u32[]{:S(2)}) copy-start(s32[2048]{0:T(1024)} %param.34) | copy-start | bytes 24580
  341.5 25.6 %all-to-all-start.3 = ((f32[32,1,1152]{2,1,0:T(1,128)}), f32[32,1,1152]{2,1,0:T(1,128)S(1)}, u32[]{:S(2)}, u32[]{:S(2)}) async-start(f32[32,1,1152]{2,1,0:T(1,128)} %reshape.581), calls=%async_computation.3 | async-start | bytes 294912 | tf_op jit(solution)/shard_map/all_to_all | solution.py:225
Sparse Core Ops, SparseCore 0:
  10.1 108.1 all-gather.8
  206.9 117.9 all-gather.6

commit v7 on v6

--- a/solution.py
+++ b/solution.py
@@ -130,10 +130,10 @@
     order = jnp.transpose(local_pages, (1, 2, 0))
     send_keys = jnp.take(pool_keys, order, axis=1)
     send_values = jnp.take(pool_values, order, axis=1)
-    got_keys, got_values = (
-        lax.all_to_all(send_keys, "group", split_axis=3, concat_axis=3, tiled=True),
-        lax.all_to_all(send_values, "group", split_axis=3, concat_axis=3, tiled=True),
-    )
+    got_pages = lax.all_to_all(
+        jnp.stack((send_keys, send_values)), "group", split_axis=4, concat_axis=4, tiled=True
+    )
+    got_keys, got_values = got_pages[0], got_pages[1]
     cache_rows = got_keys.shape[2] * got_keys.shape[3] * got_keys.shape[4]
     cache_keys = got_keys.reshape(2, SEQ_G, cache_rows, heads_dev, head_size)
     cache_values = got_values.reshape(2, SEQ_G, cache_rows, heads_dev, head_size).astype(

time: 402 us -> 402 us (level)
  waiting for transfers between devices: 202 us -> 209 us
  starting transfers between devices: 37.4 us -> 32.5 us
    all_gather x1, waiting for transfers between devices: 0.01 us -> 17.2 us  [shards(): lax.all_gather(jnp.concatenate((qkv_local.reshape(2, parts * rows_here, l...]
    all_to_all x2 -> x1, waiting for transfers between devices: 70.2 us -> 60.8 us  [shards(): lax.all_to_all(jnp.stack((send_keys, send_values)), 'group', split_axis=4...]
    all_to_all x2 -> x1, starting transfers between devices: 21.3 us -> 16.7 us  [shards(): lax.all_to_all(jnp.stack((send_keys, send_values)), 'group', split_axis=4...]
  transfers between devices with their start and end apart: 6 -> 5, of which waited for: 4 -> 4; matrix products, arithmetic and copies ran while one was open for 6% -> 6% of each run, Pallas kernels for 0% -> 0%
where the time goes in v7:
time: 402 us; the launch traced here: 396 us
  waiting for transfers between devices  209 us (52%)
  blocking collectives  80 us (20%)
  starting transfers between devices  32.5 us (8%)
  local copies, waits for them, and re-layouts  30.2 us (8%)
  matrix products  17.2 us (4%)
  between operations  14.6 us (4%)
  other arithmetic  12.8 us (3%)
    all_gather x1, waiting for transfers between devices, shards(): lax.all_gather(final, 'group', axis=1, tiled=True)  116 us
    all_to_all x1, waiting for transfers between devices, shards(): lax.all_to_all(jnp.stack((send_keys, send_values)), 'group', split_axis=4...  60.8 us
    all_gather x1, blocking collectives, shards(): lax.all_gather(jnp.stack((jnp.sum(query_raw * query_raw, axis=-1), jnp.su...  23.7 us
    all_gather x1, blocking collectives, shards(): attended_all = lax.all_gather(attended, 'vocab', axis=2, tiled=True)  18.9 us
    all_gather x1, blocking collectives, shards(): lax.all_gather(mixed_block.astype(jnp.bfloat16), 'vocab', axis=2, tiled=T...  18.8 us
    all_gather x1, blocking collectives, shards(): lax.all_gather(jnp.stack((peak_one, mass_one, target_one), axis=0), 'vocab')  18.6 us
    all_gather x1, waiting for transfers between devices, shards(): lax.all_gather(jnp.concatenate((qkv_local.reshape(2, parts * rows_here, l...  17.2 us
    all_to_all x1, starting transfers between devices, shards(): lax.all_to_all(jnp.stack((send_keys, send_values)), 'group', split_axis=4...  16.7 us
  transfers between devices with their start and end apart: 5, of which 4 were waited for; matrix products, arithmetic and copies ran while one was open for 6% of the time, Pallas kernels for 0%

profile of v7, /device:TPU:1, one launch (start us, length us, event | category | flops | bytes accessed | tf_op | source)
XLA Modules:
  0.0 396.3 jit_solution(717186836149280329)
XLA Ops:
  14.8 1.7 gather_fusion.3
  16.6 1.7 gather_fusion.4
  18.7 1.3 copy.119
  19.9 16.7 %all-to-all-start = ((bf16[2,2,2,1,32,16,128]{6,5,2,1,3,0,4:T(8,128)(2,1)}), bf16[2,2,2,1,32,16,128]{6,5,2,1,3,0,4:T(8,128)(2,1)S(1)}, u32[]{:S(2)}, u32[]{:S(2)}) async-start(bf16[2,2,2,1,32,16,128]{6,5,2,1,3,0,4:T(8,128)(2,1)} %copy.119), calls=%async_computation | async-start | bytes 2097152 | tf_op jit(solution)/shard_map/all_to_all | solution.py:133
  36.7 2.0 reshape.486
  39.8 60.8 %all-to-all-done = bf16[2,2,2,1,32,16,128]{6,5,2,1,3,0,4:T(8,128)(2,1)S(1)} async-done(((bf16[2,2,2,1,32,16,128]{6,5,2,1,3,0,4:T(8,128)(2,1)}), bf16[2,2,2,1,32,16,128]{6,5,2,1,3,0,4:T(8,128)(2,1)S(1)}, u32[]{:S(2)}, u32[]{:S(2)}) %all-to-all-start) | async-done | bytes 1048608 | tf_op jit(solution)/shard_map/all_to_all | solution.py:133
  102.5 17.2 %all-gather.9.cloned.1.call-done = bf16[64,256,128]{2,1,0:T(8,128)(2,1)} async-done(((bf16[2,256,128]{2,1,0:T(8,128)(2,1)}), bf16[64,256,128]{2,1,0:T(8,128)(2,1)}) %all-gather.9.cloned.1.call-update) | async-done | bytes 4194320 | tf_op jit(solution)/shard_map/all_gather | solution.py:83
  119.6 1.3 slice.117
  121.0 3.9 slice.107
  124.9 1.9 reshape_reshape.3
  126.7 2.7 copy.127
  129.4 6.6 %all-to-all-start.1 = ((bf16[16,2,128,128]{2,3,1,0:T(8,128)(2,1)}), bf16[16,2,128,128]{2,3,1,0:T(8,128)(2,1)S(1)}, u32[]{:S(2)}, u32[]{:S(2)}) async-start(bf16[16,2,128,128]{2,3,1,0:T(8,128)(2,1)} %bitcast.54), calls=%async_computation.1 | async-start | bytes 2097152 | tf_op jit(solution)/shard_map/all_to_all | solution.py:179
  136.1 3.2 fusion
  139.5 23.7 %all-gather.1 = f32[32,2,64]{2,1,0:T(2,128)S(1)} all-gather(f32[2,2,64]{2,1,0:T(2,128)S(1)} %pad_maximum_fusion.6), channel_id=3, replica_groups=mesh['group'=32,'vocab'=16] {'vocab'}, dimensions={0}, use_global_device_ids=true | all-gather | bytes 17408 | tf_op jit(solution)/shard_map/all_gather | solution.py:100
  165.2 18.9 %all-gather.2 = bf16[2,64,1,2048]{3,1,0,2:T(8,128)(2,1)} all-gather(bf16[2,64,1,128]{3,1,0,2:T(8,128)(2,1)S(1)} %fusion.13), channel_id=4, replica_groups=mesh['group'=32,'vocab'=16] {'vocab'}, dimensions={3}, use_global_device_ids=true | all-gather | bytes 557056 | tf_op jit(solution)/shard_map/all_gather | solution.py:181
  184.1 1.3 copy.128
  185.4 1.7 convolution_convert_fusion
  187.1 18.8 %all_gather.32 = bf16[2,64,2048]{2,1,0:T(8,128)(2,1)S(1)} all-gather(bf16[2,64,128]{2,1,0:T(8,128)(2,1)S(1)} %convolution_convert_fusion), channel_id=1, replica_groups=mesh['group'=32,'vocab'=16] {'vocab'}, dimensions={2}, use_global_device_ids=true | all-gather | bytes 557056 | tf_op jit(solution)/shard_map/all_gather | solution.py:185
  209.5 115.8 %all-gather.7.cloned.1.call-done = bf16[2,2048,2048]{2,1,0:T(8,128)(2,1)} async-done(((bf16[2,64,2048]{2,1,0:T(8,128)(2,1)}), bf16[2,2048,2048]{2,1,0:T(8,128)(2,1)}) %all-gather.7.cloned.1.call-update) | async-done | bytes 16777232 | tf_op jit(solution)/shard_map/all_gather | solution.py:197
  325.3 11.1 %fusion.79 = (f32[2,2048]{1,0:T(2,128)S(1)}, f32[2,2048,196]{1,2,0:T(8,128)}) fusion(bf16[2,2048,2048]{2,1,0:T(8,128)(2,1)} %all-gather.7.cloned.1.call-done, bf16[2,2048,196]{1,0,2:T(2,128)(2,1)S(1)} %copy-done), kind=kOutput, calls=%fused_computation.189 | convolution fusion | flops 3289133056 | bytes 21610496 | tf_op jit(solution)/shard_map/mtd,mdv->mtv/dot_general | solution.py:195
  336.5 2.8 exponential_reduce_fusion
  341.9 9.1 %all-to-all-start.2 = ((f32[32,1,1152]{2,1,0:T(1,128)}), f32[32,1,1152]{2,1,0:T(1,128)S(1)}, u32[]{:S(2)}, u32[]{:S(2)}) async-start(f32[32,1,1152]{2,1,0:T(1,128)} %reshape.579), calls=%async_computation.2 | async-start | bytes 294912 | tf_op jit(solution)/shard_map/all_to_all | solution.py:225
  352.3 15.2 %all-to-all-done.2 = f32[32,1,1152]{2,1,0:T(1,128)S(1)} async-done(((f32[32,1,1152]{2,1,0:T(1,128)}), f32[32,1,1152]{2,1,0:T(1,128)S(1)}, u32[]{:S(2)}, u32[]{:S(2)}) %all-to-all-start.2) | async-done | bytes 147488 | tf_op jit(solution)/shard_map/all_to_all | solution.py:225
  369.4 18.6 %all-gather.3 = f32[48,3,2,64]{3,2,1,0:T(2,128)S(1)} all-gather(f32[3,3,2,64]{3,2,1,0:T(2,128)S(1)} %pad_maximum_fusion.5), channel_id=5, replica_groups=mesh['group'=32,'vocab'=16] {'vocab'}, dimensions={0}, use_global_device_ids=true | all-gather | bytes 78336 | tf_op jit(solution)/shard_map/all_gather | solution.py:229
  (131 shorter events, 23.6 us)
Async XLA Ops:
  7.2 318.1 %copy-start = (bf16[2,2048,196]{1,0,2:T(2,128)(2,1)S(1)}, bf16[2,2048,196]{1,0,2:T(2,128)(2,1)}, u32[]{:S(2)}) copy-start(bf16[2,2048,196]{1,0,2:T(2,128)(2,1)} %param.27) | copy-start | bytes 4816900
  7.2 112.5 %all-gather.9.cloned.1.call-start = ((), (), s32[]{:S(2)}) async-start(), calls=%async_computation.4 | async-start | bytes 4325376 | tf_op jit(solution)/shard_map/all_gather | solution.py:83
  18.5 18.2 %copy-start.1 = (bf16[2,64,2048]{2,1,0:T(8,128)(2,1)S(1)}, bf16[2,64,2048]{2,1,0:T(8,128)(2,1)}, u32[]{:S(2)}) copy-start(bf16[2,64,2048]{2,1,0:T(8,128)(2,1)} %param.20) | copy-start | bytes 1572868
  18.6 20.1 %copy-start.10 = (s32[64]{0:T(128)S(1)}, s32[64]{0:T(128)}, u32[]{:S(2)}) copy-start(s32[64]{0:T(128)} %param.31) | copy-start | bytes 772
  18.6 20.2 %copy-start.9 = (s32[32,64]{1,0:T(8,128)S(1)}, s32[32,64]{1,0:T(8,128)}, u32[]{:S(2)}) copy-start(s32[32,64]{1,0:T(8,128)} %param.33) | copy-start | bytes 24580
  18.6 20.2 %copy-start.11 = (s32[64]{0:T(128)S(1)}, s32[64]{0:T(128)}, u32[]{:S(2)}) copy-start(s32[64]{0:T(128)} %param.32) | copy-start | bytes 772
  19.9 80.6 %all-to-all-start = ((bf16[2,2,2,1,32,16,128]{6,5,2,1,3,0,4:T(8,128)(2,1)}), bf16[2,2,2,1,32,16,128]{6,5,2,1,3,0,4:T(8,128)(2,1)S(1)}, u32[]{:S(2)}, u32[]{:S(2)}) async-start(bf16[2,2,2,1,32,16,128]{6,5,2,1,3,0,4:T(8,128)(2,1)} %copy.119), calls=%async_computation | async-start | bytes 2097152 | tf_op jit(solution)/shard_map/all_to_all | solution.py:133
  129.4 54.6 %all-to-all-start.1 = ((bf16[16,2,128,128]{2,3,1,0:T(8,128)(2,1)}), bf16[16,2,128,128]{2,3,1,0:T(8,128)(2,1)S(1)}, u32[]{:S(2)}, u32[]{:S(2)}) async-start(bf16[16,2,128,128]{2,3,1,0:T(8,128)(2,1)} %bitcast.54), calls=%async_computation.1 | async-start | bytes 2097152 | tf_op jit(solution)/shard_map/all_to_all | solution.py:179
  136.0 27.3 %copy-start.7 = (f32[2,128]{1,0:T(2,128)S(1)}, f32[2,128]{1,0:T(2,128)}, u32[]{:S(2)}) copy-start(f32[2,128]{1,0:T(2,128)} %param.23) | copy-start | bytes 3076
  136.0 27.3 %copy-start.8 = (f32[2,128]{1,0:T(2,128)S(1)}, f32[2,128]{1,0:T(2,128)}, u32[]{:S(2)}) copy-start(f32[2,128]{1,0:T(2,128)} %param.24) | copy-start | bytes 3076
  136.0 189.2 %all-gather.7.cloned.1.call-start = ((), (), s32[]{:S(2)}) async-start(), calls=%async_computation.3 | async-start | bytes 17301504 | tf_op jit(solution)/shard_map/all_gather | solution.py:197
  136.1 27.6 %copy-start.3 = (bf16[1,2,2,1,32,16,128]{6,5,4,2,1,3,0:T(8,128)(2,1)S(1)}, bf16[1,2,2,1,32,16,128]{6,5,4,2,1,3,0:T(8,128)(2,1)}, u32[]{:S(2)}) copy-start(bf16[1,2,2,1,32,16,128]{6,5,4,2,1,3,0:T(8,128)(2,1)} %copy.121) | copy-start | bytes 1572868
  139.3 25.3 %copy-start.2 = (bf16[1,2,2,1,32,16,128]{6,5,4,2,1,3,0:T(8,128)(2,1)S(1)}, bf16[1,2,2,1,32,16,128]{6,5,4,2,1,3,0:T(8,128)(2,1)}, u32[]{:S(2)}) copy-start(bf16[1,2,2,1,32,16,128]{6,5,4,2,1,3,0:T(8,128)(2,1)} %copy.120) | copy-start | bytes 1572868
  164.7 41.5 %copy-start.4 = (f32[2,2048]{1,0:T(2,128)S(1)}, f32[2,2048]{1,0:T(2,128)}, u32[]{:S(2)}) copy-start(f32[2,2048]{1,0:T(2,128)} %param.25) | copy-start | bytes 49156
  184.0 22.5 %copy-start.5 = (f32[2,2048]{1,0:T(2,128)S(1)}, f32[2,2048]{1,0:T(2,128)}, u32[]{:S(2)}) copy-start(f32[2,2048]{1,0:T(2,128)} %param.26) | copy-start | bytes 49156
  185.4 23.9 %copy-start.6 = (s32[2048]{0:T(1024)S(1)}, s32[2048]{0:T(1024)}, u32[]{:S(2)}) copy-start(s32[2048]{0:T(1024)} %param.34) | copy-start | bytes 24580
  341.9 25.6 %all-to-all-start.2 = ((f32[32,1,1152]{2,1,0:T(1,128)}), f32[32,1,1152]{2,1,0:T(1,128)S(1)}, u32[]{:S(2)}, u32[]{:S(2)}) async-start(f32[32,1,1152]{2,1,0:T(1,128)} %reshape.579), calls=%async_computation.2 | async-start | bytes 294912 | tf_op jit(solution)/shard_map/all_to_all | solution.py:225
Sparse Core Ops, SparseCore 0:
  10.1 109.4 all-gather.8
  207.7 117.5 all-gather.6

commit v8 on v7

--- a/solution.py
+++ b/solution.py
@@ -80,12 +80,18 @@
     parts = qkv_weight.shape[2] // lane
     rows_here = qkv_weight.shape[1]
     qkv_local = jnp.transpose(qkv_weight.reshape(2, rows_here, parts, lane), (0, 2, 1, 3))
-    both_weights = lax.all_gather(
-        jnp.concatenate(
-            (qkv_local.reshape(2, parts * rows_here, lane), out_weight.reshape(2, -1, lane)), axis=1
-        ),
-        "group",
-    )
+    both_weights = jnp.concatenate(
+        (qkv_local.reshape(2, parts * rows_here, lane), out_weight.reshape(2, -1, lane)), axis=1
+    )[None]
+    step = 1
+    while step < groups:
+        other = lax.ppermute(both_weights, "group", [(i, i ^ step) for i in range(groups)])
+        both_weights = jnp.where(
+            (group_idx // step) % 2 == 0,
+            jnp.concatenate((both_weights, other)),
+            jnp.concatenate((other, both_weights)),
+        )
+        step *= 2
     qkv_rows = both_weights[:, :, : parts * rows_here].reshape(groups, 2, parts, rows_here, lane)
     out_rows = both_weights[:, :, parts * rows_here :].reshape((groups,) + out_weight.shape)
     united = jnp.einsum(

time: 402 us -> 717 us (1.78)
  waiting for transfers between devices: 209 us -> 401 us
  starting transfers between devices: 32.5 us -> 152 us
  other arithmetic: 12.8 us -> 22.2 us
    ppermute x0 -> x5, waiting for transfers between devices: none -> 273 us  [shards(): lax.ppermute(both_weights, 'group', [(i, i ^ step) for i in range(groups)])]
    all_to_all x1, starting transfers between devices: 6.57 us -> 106 us  [shards(): lax.all_to_all(head_rows, 'vocab', split_axis=0, concat_axis=0, tiled=True)]
    all_to_all x1, waiting for transfers between devices: 60.8 us -> 0.01 us  [shards(): lax.all_to_all(jnp.stack((send_keys, send_values)), 'group', split_axis=4...]
    ppermute x0 -> x5, starting transfers between devices: none -> 24.4 us  [shards(): lax.ppermute(both_weights, 'group', [(i, i ^ step) for i in range(groups)])]
    all_gather x1 -> x0, waiting for transfers between devices: 17.2 us -> none  [shards(): lax.all_gather(jnp.concatenate((qkv_local.reshape(2, parts * rows_here, l...]
    select_n x0 -> x5, other arithmetic: none -> 9.99 us  [shards(): jnp.where(group_idx // step % 2 == 0, jnp.concatenate((both_weights, othe...]
  transfers between devices with their start and end apart: 5 -> 9, of which waited for: 4 -> 6; matrix products, arithmetic and copies ran while one was open for 6% -> 5% of each run, Pallas kernels for 0% -> 0%
where the time goes in v8:
time: 717 us; the launch traced here: 711 us
  waiting for transfers between devices  401 us (56%)
  starting transfers between devices  152 us (21%)
  blocking collectives  78.7 us (11%)
  local copies, waits for them, and re-layouts  26.4 us (4%)
  other arithmetic  22.2 us (3%)
  matrix products  16.2 us (2%)
  between operations  14.8 us (2%)
    ppermute x5, waiting for transfers between devices, shards(): lax.ppermute(both_weights, 'group', [(i, i ^ step) for i in range(groups)])  273 us
    all_gather x1, waiting for transfers between devices, shards(): lax.all_gather(final, 'group', axis=1, tiled=True)  113 us
    all_to_all x1, starting transfers between devices, shards(): lax.all_to_all(head_rows, 'vocab', split_axis=0, concat_axis=0, tiled=True)  106 us
    ppermute x5, starting transfers between devices, shards(): lax.ppermute(both_weights, 'group', [(i, i ^ step) for i in range(groups)])  24.4 us
    all_gather x1, blocking collectives, shards(): lax.all_gather(jnp.stack((jnp.sum(query_raw * query_raw, axis=-1), jnp.su...  22.5 us
    all_gather x1, blocking collectives, shards(): attended_all = lax.all_gather(attended, 'vocab', axis=2, tiled=True)  20.3 us
    all_gather x1, blocking collectives, shards(): lax.all_gather(jnp.stack((peak_one, mass_one, target_one), axis=0), 'vocab')  18.6 us
    all_gather x1, blocking collectives, shards(): lax.all_gather(mixed_block.astype(jnp.bfloat16), 'vocab', axis=2, tiled=T...  17.4 us
  transfers between devices with their start and end apart: 9, of which 6 were waited for; matrix products, arithmetic and copies ran while one was open for 5% of the time, Pallas kernels for 0%

profile of v8, /device:TPU:1, one launch (start us, length us, event | category | flops | bytes accessed | tf_op | source)
XLA Modules:
  0.0 711.0 jit_solution(2576581212542581264)
XLA Ops:
  9.3 8.7 %collective-permute-start = (bf16[1,2,256,128]{3,2,1,0:T(8,128)(2,1)S(1)}, bf16[1,2,256,128]{3,2,1,0:T(8,128)(2,1)S(1)}, u32[]{:S(2)}, u32[]{:S(2)}) collective-permute-start(bf16[1,2,256,128]{3,2,1,0:T(8,128)(2,1)S(1)} %maximum_bitcast_fusion), channel_id=1, source_target_pairs={{0,16},{16,0},{32,48},{48,32},{64,80},{80,64},{96,112},{112,96},{1... | collective-permute-start | bytes 393224 | tf_op jit(solution)/shard_map/ppermute | solution.py:88
  27.4 5.4 collective-permute-done.1
  37.4 12.3 %all-to-all-start = ((bf16[2,2,2,1,32,16,128]{6,5,2,1,3,0,4:T(8,128)(2,1)}), bf16[2,2,2,1,32,16,128]{6,5,2,1,3,0,4:T(8,128)(2,1)}, u32[]{:S(2)}, u32[]{:S(2)}) async-start(bf16[2,2,2,1,32,16,128]{6,5,2,1,3,0,4:T(8,128)(2,1)} %copy.119), calls=%async_computation | async-start | bytes 2097152 | tf_op jit(solution)/shard_map/all_to_all | solution.py:139
  49.8 38.3 %collective-permute-done.2 = bf16[4,2,256,128]{3,2,1,0:T(8,128)(2,1)} collective-permute-done((bf16[4,2,256,128]{3,2,1,0:T(8,128)(2,1)S(1)}, bf16[4,2,256,128]{3,2,1,0:T(8,128)(2,1)}, u32[]{:S(2)}, u32[]{:S(2)}) %collective-permute-start.2) | collective-permute-done | bytes 524320 | tf_op jit(solution)/shard_map/ppermute | solution.py:88
  89.8 2.1 collective-permute-start.3
  91.9 149.7 %collective-permute-done.3 = bf16[8,2,256,128]{3,2,1,0:T(8,128)(2,1)} collective-permute-done((bf16[8,2,256,128]{3,2,1,0:T(8,128)(2,1)S(1)}, bf16[8,2,256,128]{3,2,1,0:T(8,128)(2,1)}, u32[]{:S(2)}, u32[]{:S(2)}) %collective-permute-start.3) | collective-permute-done | bytes 1048608 | tf_op jit(solution)/shard_map/ppermute | solution.py:88
  241.6 3.3 maximum_select_fusion.1
  245.0 9.7 %collective-permute-start.4 = (bf16[16,2,256,128]{3,2,1,0:T(8,128)(2,1)}, bf16[16,2,256,128]{3,2,1,0:T(8,128)(2,1)}, u32[]{:S(2)}, u32[]{:S(2)}) collective-permute-start(bf16[16,2,256,128]{3,2,1,0:T(8,128)(2,1)} %maximum_select_fusion.1), channel_id=1, source_target_pairs={{0,256},{16,272},{32,288},{48,304},{64,320},{80,336},{96,352},{112... | collective-permute-start | bytes 6291464 | tf_op jit(solution)/shard_map/ppermute | solution.py:88
  254.7 2.0 reshape.486
  257.8 79.2 %collective-permute-done.4 = bf16[16,2,256,128]{3,2,1,0:T(8,128)(2,1)} collective-permute-done((bf16[16,2,256,128]{3,2,1,0:T(8,128)(2,1)}, bf16[16,2,256,128]{3,2,1,0:T(8,128)(2,1)}, u32[]{:S(2)}, u32[]{:S(2)}) %collective-permute-start.4) | collective-permute-done | bytes 2097184 | tf_op jit(solution)/shard_map/ppermute | solution.py:88
  337.0 3.8 maximum_select_fusion
  340.9 2.0 slice.107
  344.7 2.8 copy.127
  347.4 105.7 %all-to-all-start.1 = ((bf16[16,2,128,128]{2,3,1,0:T(8,128)(2,1)}), bf16[16,2,128,128]{2,3,1,0:T(8,128)(2,1)S(1)}, u32[]{:S(2)}, u32[]{:S(2)}) async-start(bf16[16,2,128,128]{2,3,1,0:T(8,128)(2,1)} %bitcast.54), calls=%async_computation.1 | async-start | bytes 2097152 | tf_op jit(solution)/shard_map/all_to_all | solution.py:185
  455.4 2.2 fusion
  457.8 22.5 %all-gather = f32[32,2,64]{2,1,0:T(2,128)S(1)} all-gather(f32[2,2,64]{2,1,0:T(2,128)S(1)} %pad_maximum_fusion.5), channel_id=2, replica_groups=mesh['group'=32,'vocab'=16] {'vocab'}, dimensions={0}, use_global_device_ids=true | all-gather | bytes 17408 | tf_op jit(solution)/shard_map/all_gather | solution.py:106
  482.3 20.3 %all-gather.1 = bf16[2,64,1,2048]{3,1,0,2:T(8,128)(2,1)} all-gather(bf16[2,64,1,128]{3,1,0,2:T(8,128)(2,1)S(1)} %fusion.13), channel_id=3, replica_groups=mesh['group'=32,'vocab'=16] {'vocab'}, dimensions={3}, use_global_device_ids=true | all-gather | bytes 557056 | tf_op jit(solution)/shard_map/all_gather | solution.py:187
  505.7 17.4 %all_gather.24 = bf16[2,64,2048]{2,1,0:T(8,128)(2,1)S(1)} all-gather(bf16[2,64,128]{2,1,0:T(8,128)(2,1)S(1)} %convolution_convert_fusion), channel_id=1, replica_groups=mesh['group'=32,'vocab'=16] {'vocab'}, dimensions={2}, use_global_device_ids=true | all-gather | bytes 557056 | tf_op jit(solution)/shard_map/all_gather | solution.py:191
  526.6 113.4 %all-gather.5.cloned.1.call-done = bf16[2,2048,2048]{2,1,0:T(8,128)(2,1)} async-done(((bf16[2,64,2048]{2,1,0:T(8,128)(2,1)}), bf16[2,2048,2048]{2,1,0:T(8,128)(2,1)}) %all-gather.5.cloned.1.call-update) | async-done | bytes 16777232 | tf_op jit(solution)/shard_map/all_gather | solution.py:203
  640.0 11.1 %fusion.79 = (f32[2,2048]{1,0:T(2,128)S(1)}, f32[2,2048,196]{1,2,0:T(8,128)}) fusion(bf16[2,2048,2048]{2,1,0:T(8,128)(2,1)} %all-gather.5.cloned.1.call-done, bf16[2,2048,196]{1,0,2:T(2,128)(2,1)S(1)} %copy-done), kind=kOutput, calls=%fused_computation.194 | convolution fusion | flops 3289133056 | bytes 21610496 | tf_op jit(solution)/shard_map/mtd,mdv->mtv/dot_general | solution.py:201
  651.2 2.8 exponential_reduce_fusion
  656.6 9.1 %all-to-all-start.2 = ((f32[32,1,1152]{2,1,0:T(1,128)}), f32[32,1,1152]{2,1,0:T(1,128)S(1)}, u32[]{:S(2)}, u32[]{:S(2)}) async-start(f32[32,1,1152]{2,1,0:T(1,128)} %reshape.578), calls=%async_computation.2 | async-start | bytes 294912 | tf_op jit(solution)/shard_map/all_to_all | solution.py:231
  666.9 15.2 %all-to-all-done.2 = f32[32,1,1152]{2,1,0:T(1,128)S(1)} async-done(((f32[32,1,1152]{2,1,0:T(1,128)}), f32[32,1,1152]{2,1,0:T(1,128)S(1)}, u32[]{:S(2)}, u32[]{:S(2)}) %all-to-all-start.2) | async-done | bytes 147488 | tf_op jit(solution)/shard_map/all_to_all | solution.py:231
  684.1 18.6 %all-gather.2 = f32[48,3,2,64]{3,2,1,0:T(2,128)S(1)} all-gather(f32[3,3,2,64]{3,2,1,0:T(2,128)S(1)} %pad_maximum_fusion.4), channel_id=4, replica_groups=mesh['group'=32,'vocab'=16] {'vocab'}, dimensions={0}, use_global_device_ids=true | all-gather | bytes 78336 | tf_op jit(solution)/shard_map/all_gather | solution.py:235
  (145 shorter events, 38.6 us)
Async XLA Ops:
  7.2 632.8 %copy-start = (bf16[2,2048,196]{1,0,2:T(2,128)(2,1)S(1)}, bf16[2,2048,196]{1,0,2:T(2,128)(2,1)}, u32[]{:S(2)}) copy-start(bf16[2,2048,196]{1,0,2:T(2,128)(2,1)} %param.27) | copy-start | bytes 4816900
  7.2 19.5 %copy-start.4 = (bf16[2,64,16,128]{3,2,1,0:T(8,128)(2,1)S(1)}, bf16[2,64,16,128]{3,2,1,0:T(8,128)(2,1)}, u32[]{:S(2)}) copy-start(bf16[2,64,16,128]{3,2,1,0:T(8,128)(2,1)} %param.29) | copy-start | bytes 1572868
  9.3 13.6 %collective-permute-start = (bf16[1,2,256,128]{3,2,1,0:T(8,128)(2,1)S(1)}, bf16[1,2,256,128]{3,2,1,0:T(8,128)(2,1)S(1)}, u32[]{:S(2)}, u32[]{:S(2)}) collective-permute-start(bf16[1,2,256,128]{3,2,1,0:T(8,128)(2,1)S(1)} %maximum_bitcast_fusion), channel_id=1, source_target_pairs={{0,16},{16,0},{32,48},{48,32},{64,80},{80,64},{96,112},{112,96},{1... | collective-permute-start | bytes 393224 | tf_op jit(solution)/shard_map/ppermute | solution.py:88
  22.9 9.8 %collective-permute-start.1 = (bf16[2,2,256,128]{3,2,1,0:T(8,128)(2,1)S(1)}, bf16[2,2,256,128]{3,2,1,0:T(8,128)(2,1)}, u32[]{:S(2)}, u32[]{:S(2)}) collective-permute-start(bf16[2,2,256,128]{3,2,1,0:T(8,128)(2,1)S(1)} %maximum_select_fusion.4), channel_id=1, source_target_pairs={{0,32},{16,48},{32,0},{48,16},{64,96},{80,112},{96,64},{112,80},{1... | collective-permute-start | bytes 786440 | tf_op jit(solution)/shard_map/ppermute | solution.py:88
  33.9 3.5 copy-start.3
  33.9 54.2 %collective-permute-start.2 = (bf16[4,2,256,128]{3,2,1,0:T(8,128)(2,1)S(1)}, bf16[4,2,256,128]{3,2,1,0:T(8,128)(2,1)}, u32[]{:S(2)}, u32[]{:S(2)}) collective-permute-start(bf16[4,2,256,128]{3,2,1,0:T(8,128)(2,1)S(1)} %maximum_select_fusion.3), channel_id=1, source_target_pairs={{0,64},{16,80},{32,96},{48,112},{64,0},{80,16},{96,32},{112,48},{1... | collective-permute-start | bytes 1572872 | tf_op jit(solution)/shard_map/ppermute | solution.py:88
  37.4 310.0 %all-to-all-start = ((bf16[2,2,2,1,32,16,128]{6,5,2,1,3,0,4:T(8,128)(2,1)}), bf16[2,2,2,1,32,16,128]{6,5,2,1,3,0,4:T(8,128)(2,1)}, u32[]{:S(2)}, u32[]{:S(2)}) async-start(bf16[2,2,2,1,32,16,128]{6,5,2,1,3,0,4:T(8,128)(2,1)} %copy.119), calls=%async_computation | async-start | bytes 2097152 | tf_op jit(solution)/shard_map/all_to_all | solution.py:139
  49.8 205.0 %copy-start.2 = (bf16[2,64,2048]{2,1,0:T(8,128)(2,1)S(1)}, bf16[2,64,2048]{2,1,0:T(8,128)(2,1)}, u32[]{:S(2)}) copy-start(bf16[2,64,2048]{2,1,0:T(8,128)(2,1)} %param.20) | copy-start | bytes 1572868
  89.8 167.0 %copy-start.11 = (s32[64]{0:T(128)S(1)}, s32[64]{0:T(128)}, u32[]{:S(2)}) copy-start(s32[64]{0:T(128)} %param.31) | copy-start | bytes 772
  89.8 167.1 %copy-start.10 = (s32[32,64]{1,0:T(8,128)S(1)}, s32[32,64]{1,0:T(8,128)}, u32[]{:S(2)}) copy-start(s32[32,64]{1,0:T(8,128)} %param.33) | copy-start | bytes 24580
  89.8 167.1 %copy-start.12 = (s32[64]{0:T(128)S(1)}, s32[64]{0:T(128)}, u32[]{:S(2)}) copy-start(s32[64]{0:T(128)} %param.32) | copy-start | bytes 772
  89.8 151.8 %collective-permute-start.3 = (bf16[8,2,256,128]{3,2,1,0:T(8,128)(2,1)S(1)}, bf16[8,2,256,128]{3,2,1,0:T(8,128)(2,1)}, u32[]{:S(2)}, u32[]{:S(2)}) collective-permute-start(bf16[8,2,256,128]{3,2,1,0:T(8,128)(2,1)S(1)} %maximum_select_fusion.2), channel_id=1, source_target_pairs={{0,128},{16,144},{32,160},{48,176},{64,192},{80,208},{96,224},{112... | collective-permute-start | bytes 3145736 | tf_op jit(solution)/shard_map/ppermute | solution.py:88
  245.0 92.0 %collective-permute-start.4 = (bf16[16,2,256,128]{3,2,1,0:T(8,128)(2,1)}, bf16[16,2,256,128]{3,2,1,0:T(8,128)(2,1)}, u32[]{:S(2)}, u32[]{:S(2)}) collective-permute-start(bf16[16,2,256,128]{3,2,1,0:T(8,128)(2,1)} %maximum_select_fusion.1), channel_id=1, source_target_pairs={{0,256},{16,272},{32,288},{48,304},{64,320},{80,336},{96,352},{112... | collective-permute-start | bytes 6291464 | tf_op jit(solution)/shard_map/ppermute | solution.py:88
  347.4 155.2 %all-to-all-start.1 = ((bf16[16,2,128,128]{2,3,1,0:T(8,128)(2,1)}), bf16[16,2,128,128]{2,3,1,0:T(8,128)(2,1)S(1)}, u32[]{:S(2)}, u32[]{:S(2)}) async-start(bf16[16,2,128,128]{2,3,1,0:T(8,128)(2,1)} %bitcast.54), calls=%async_computation.1 | async-start | bytes 2097152 | tf_op jit(solution)/shard_map/all_to_all | solution.py:185
  453.2 186.8 %all-gather.5.cloned.1.call-start = ((), (), s32[]{:S(2)}) async-start(), calls=%async_computation.3 | async-start | bytes 17301504 | tf_op jit(solution)/shard_map/all_gather | solution.py:203
  453.2 2.2 copy-start.1
  455.4 24.9 %copy-start.8 = (f32[2,128]{1,0:T(2,128)S(1)}, f32[2,128]{1,0:T(2,128)}, u32[]{:S(2)}) copy-start(f32[2,128]{1,0:T(2,128)} %param.23) | copy-start | bytes 3076
  455.4 24.9 %copy-start.9 = (f32[2,128]{1,0:T(2,128)S(1)}, f32[2,128]{1,0:T(2,128)}, u32[]{:S(2)}) copy-start(f32[2,128]{1,0:T(2,128)} %param.24) | copy-start | bytes 3076
  482.1 41.2 %copy-start.5 = (f32[2,2048]{1,0:T(2,128)S(1)}, f32[2,2048]{1,0:T(2,128)}, u32[]{:S(2)}) copy-start(f32[2,2048]{1,0:T(2,128)} %param.25) | copy-start | bytes 49156
  502.6 21.1 %copy-start.6 = (f32[2,2048]{1,0:T(2,128)S(1)}, f32[2,2048]{1,0:T(2,128)}, u32[]{:S(2)}) copy-start(f32[2,2048]{1,0:T(2,128)} %param.26) | copy-start | bytes 49156
  505.7 20.7 %copy-start.7 = (s32[2048]{0:T(1024)S(1)}, s32[2048]{0:T(1024)}, u32[]{:S(2)}) copy-start(s32[2048]{0:T(1024)} %param.34) | copy-start | bytes 24580
  656.6 25.6 %all-to-all-start.2 = ((f32[32,1,1152]{2,1,0:T(1,128)}), f32[32,1,1152]{2,1,0:T(1,128)S(1)}, u32[]{:S(2)}, u32[]{:S(2)}) async-start(f32[32,1,1152]{2,1,0:T(1,128)} %reshape.578), calls=%async_computation.2 | async-start | bytes 294912 | tf_op jit(solution)/shard_map/all_to_all | solution.py:231
Sparse Core Ops, SparseCore 0:
  524.8 115.1 all-gather.4

commit v9 on v6

--- a/solution.py
+++ b/solution.py
@@ -192,11 +192,16 @@
     final = rms_scale(hidden_new.astype(jnp.float32), final_gain[:, None, :]).astype(jnp.bfloat16)
     voc_here = head_weight.shape[2]
     first_column = (group_idx * vocab_count + vocab_idx) * voc_here
-    logits = jnp.einsum(
-        "mtd,mdv->mtv",
-        lax.all_gather(final, "group", axis=1, tiled=True),
-        head_weight,
-        preferred_element_type=jnp.float32,
+    logits = jnp.concatenate(
+        [
+            jnp.einsum(
+                "mtd,mdv->mtv",
+                lax.all_gather(final[model : model + 1], "group", axis=1, tiled=True),
+                head_weight[model : model + 1],
+                preferred_element_type=jnp.float32,
+            )
+            for model in range(2)
+        ]
     )
     highest = jnp.max(logits, axis=-1)
     exp_sum = jnp.sum(jnp.exp(logits - highest[..., None]), axis=-1)

time: 402 us -> 445 us (1.11)
  waiting for transfers between devices: 202 us -> 241 us
    all_gather x1 -> x2, waiting for transfers between devices: 116 us -> 154 us  [shards(): lax.all_gather(final[model:model + 1], 'group', axis=1, tiled=True)]
    dot_general x1 -> x2, matrix products: 11.1 us -> 13.4 us  [shards(): jnp.einsum('mtd,mdv->mtv', lax.all_gather(final[model:model + 1], 'group'...]
  transfers between devices with their start and end apart: 6 -> 7, of which waited for: 4 -> 6; matrix products, arithmetic and copies ran while one was open for 6% -> 7% of each run, Pallas kernels for 0% -> 0%
where the time goes in v9:
time: 445 us; the launch traced here: 438 us
  waiting for transfers between devices  241 us (54%)
  blocking collectives  80.9 us (18%)
  starting transfers between devices  35.7 us (8%)
  local copies, waits for them, and re-layouts  35.1 us (8%)
  matrix products  19.2 us (4%)
  between operations  14.4 us (3%)
  other arithmetic  11.7 us (3%)
    all_gather x2, waiting for transfers between devices, shards(): lax.all_gather(final[model:model + 1], 'group', axis=1, tiled=True)  154 us
    all_to_all x1, waiting for transfers between devices, shards(): lax.all_to_all(send_values, 'group', split_axis=3, concat_axis=3, tiled=T...  36.8 us
    all_to_all x1, waiting for transfers between devices, shards(): lax.all_to_all(send_keys, 'group', split_axis=3, concat_axis=3, tiled=True)  34.6 us
    all_gather x1, blocking collectives, shards(): lax.all_gather(jnp.stack((jnp.sum(query_raw * query_raw, axis=-1), jnp.su...  24.1 us
    all_gather x1, blocking collectives, shards(): attended_all = lax.all_gather(attended, 'vocab', axis=2, tiled=True)  19.6 us
    all_gather x1, blocking collectives, shards(): lax.all_gather(jnp.stack((peak_one, mass_one, target_one), axis=0), 'vocab')  18.7 us
    all_gather x1, blocking collectives, shards(): lax.all_gather(mixed_block.astype(jnp.bfloat16), 'vocab', axis=2, tiled=T...  18.4 us
    all_to_all x1, starting transfers between devices, shards(): lax.all_to_all(send_values, 'group', split_axis=3, concat_axis=3, tiled=T...  16.7 us
  transfers between devices with their start and end apart: 7, of which 6 were waited for; matrix products, arithmetic and copies ran while one was open for 7% of the time, Pallas kernels for 0%

profile of v9, /device:TPU:1, one launch (start us, length us, event | category | flops | bytes accessed | tf_op | source)
XLA Modules:
  0.0 438.4 jit_solution(2143472381784333685)
XLA Ops:
  15.5 1.7 gather_fusion.3
  18.3 16.7 %all-to-all-start = ((bf16[2,2,1,32,16,128]{5,4,1,0,2,3:T(8,128)(2,1)}), bf16[2,2,1,32,16,128]{5,4,1,0,2,3:T(8,128)(2,1)S(1)}, u32[]{:S(2)}, u32[]{:S(2)}) async-start(bf16[2,2,1,32,16,128]{5,4,1,0,2,3:T(8,128)(2,1)} %copy.123), calls=%async_computation | async-start | bytes 1048576 | tf_op jit(solution)/shard_map/all_to_all | solution.py:135
  36.0 36.8 %all-to-all-done = bf16[2,2,1,32,16,128]{5,4,1,0,2,3:T(8,128)(2,1)S(1)} async-done(((bf16[2,2,1,32,16,128]{5,4,1,0,2,3:T(8,128)(2,1)}), bf16[2,2,1,32,16,128]{5,4,1,0,2,3:T(8,128)(2,1)S(1)}, u32[]{:S(2)}, u32[]{:S(2)}) %all-to-all-start) | async-done | bytes 524320 | tf_op jit(solution)/shard_map/all_to_all | solution.py:135
  72.8 4.2 all-to-all-start.1
  77.0 2.0 reshape.502
  80.9 34.6 %all-to-all-done.1 = bf16[2,2,1,32,16,128]{5,4,1,0,2,3:T(8,128)(2,1)S(1)} async-done(((bf16[2,2,1,32,16,128]{5,4,1,0,2,3:T(8,128)(2,1)}), bf16[2,2,1,32,16,128]{5,4,1,0,2,3:T(8,128)(2,1)S(1)}, u32[]{:S(2)}, u32[]{:S(2)}) %all-to-all-start.1) | async-done | bytes 524320 | tf_op jit(solution)/shard_map/all_to_all | solution.py:134
  117.0 2.4 slice.123
  119.4 3.9 slice.113
  123.3 2.7 reshape_reshape.3
  126.1 1.6 copy.132
  127.7 6.7 %all-to-all-start.2 = ((bf16[16,2,128,128]{2,3,1,0:T(8,128)(2,1)}), bf16[16,2,128,128]{2,3,1,0:T(8,128)(2,1)S(1)}, u32[]{:S(2)}, u32[]{:S(2)}) async-start(bf16[16,2,128,128]{2,3,1,0:T(8,128)(2,1)} %bitcast.215), calls=%async_computation.2 | async-start | bytes 2097152 | tf_op jit(solution)/shard_map/all_to_all | solution.py:179
  134.5 3.2 fusion.4
  137.9 24.1 %all-gather.1 = f32[32,2,64]{2,1,0:T(2,128)S(1)} all-gather(f32[2,2,64]{2,1,0:T(2,128)S(1)} %pad_maximum_fusion.6), channel_id=3, replica_groups=mesh['group'=32,'vocab'=16] {'vocab'}, dimensions={0}, use_global_device_ids=true | all-gather | bytes 17408 | tf_op jit(solution)/shard_map/all_gather | solution.py:100
  163.9 19.6 %all-gather.2 = bf16[2,64,1,2048]{3,1,0,2:T(8,128)(2,1)} all-gather(bf16[2,64,1,128]{3,1,0,2:T(8,128)(2,1)S(1)} %fusion.22), channel_id=4, replica_groups=mesh['group'=32,'vocab'=16] {'vocab'}, dimensions={3}, use_global_device_ids=true | all-gather | bytes 557056 | tf_op jit(solution)/shard_map/all_gather | solution.py:181
  185.6 18.4 %all_gather.35 = bf16[2,64,2048]{2,1,0:T(8,128)(2,1)S(1)} all-gather(bf16[2,64,128]{2,1,0:T(8,128)(2,1)S(1)} %convolution_convert_fusion), channel_id=1, replica_groups=mesh['group'=32,'vocab'=16] {'vocab'}, dimensions={2}, use_global_device_ids=true | all-gather | bytes 557056 | tf_op jit(solution)/shard_map/all_gather | solution.py:185
  208.4 3.5 fusion.85
  211.9 82.9 %all-gather.10.cloned.1.call-done = bf16[1,2048,2048]{2,1,0:T(8,128)(2,1)} async-done(((bf16[1,64,2048]{2,1,0:T(8,128)(2,1)}), bf16[1,2048,2048]{2,1,0:T(8,128)(2,1)}) %all-gather.10.cloned.1.call-update) | async-done | bytes 8388624 | tf_op jit(solution)/shard_map/all_gather | solution.py:199
  294.8 6.7 %fusion.9 = f32[1,2048,196]{1,2,0:T(8,128)S(1)} fusion(bf16[1,2048,2048]{2,1,0:T(8,128)(2,1)} %all-gather.10.cloned.1.call-done, bf16[1,2048,196]{1,0,2:T(2,128)(2,1)} %get-tuple-element.27), kind=kOutput, calls=%fused_computation.17 | convolution fusion | flops 1644167168 | bytes 10797056 | tf_op jit(solution)/shard_map/mtd,mdv->mtv/dot_general | solution.py:197
  301.6 70.8 %all-gather.8.cloned.1.call-done = bf16[1,2048,2048]{2,1,0:T(8,128)(2,1)} async-done(((bf16[1,64,2048]{2,1,0:T(8,128)(2,1)}), bf16[1,2048,2048]{2,1,0:T(8,128)(2,1)}) %all-gather.8.cloned.1.call-update) | async-done | bytes 8388624 | tf_op jit(solution)/shard_map/all_gather | solution.py:199
  372.3 6.7 %fusion.6 = f32[1,2048,196]{1,2,0:T(8,128)S(1)} fusion(bf16[1,2048,2048]{2,1,0:T(8,128)(2,1)} %all-gather.8.cloned.1.call-done, bf16[1,2048,196]{1,0,2:T(2,128)(2,1)} %get-tuple-element.26), kind=kOutput, calls=%fused_computation.16 | convolution fusion | flops 1644167168 | bytes 10797056 | tf_op jit(solution)/shard_map/mtd,mdv->mtv/dot_general | solution.py:197
  380.6 2.3 exponential_reduce_fusion
  385.5 7.7 %all-to-all-start.3 = ((f32[32,1,1152]{2,1,0:T(1,128)}), f32[32,1,1152]{2,1,0:T(1,128)S(1)}, u32[]{:S(2)}, u32[]{:S(2)}) async-start(f32[32,1,1152]{2,1,0:T(1,128)} %reshape.599), calls=%async_computation.3 | async-start | bytes 294912 | tf_op jit(solution)/shard_map/all_to_all | solution.py:230
  394.5 15.2 %all-to-all-done.3 = f32[32,1,1152]{2,1,0:T(1,128)S(1)} async-done(((f32[32,1,1152]{2,1,0:T(1,128)}), f32[32,1,1152]{2,1,0:T(1,128)S(1)}, u32[]{:S(2)}, u32[]{:S(2)}) %all-to-all-start.3) | async-done | bytes 147488 | tf_op jit(solution)/shard_map/all_to_all | solution.py:230
  411.7 18.7 %all-gather.3 = f32[48,3,2,64]{3,2,1,0:T(2,128)S(1)} all-gather(f32[3,3,2,64]{3,2,1,0:T(2,128)S(1)} %pad_maximum_fusion.5), channel_id=5, replica_groups=mesh['group'=32,'vocab'=16] {'vocab'}, dimensions={0}, use_global_device_ids=true | all-gather | bytes 78336 | tf_op jit(solution)/shard_map/all_gather | solution.py:234
  (143 shorter events, 30.5 us)
Async XLA Ops:
  7.2 7.6 %copy-start = (bf16[2,64,16,128]{3,2,1,0:T(8,128)(2,1)S(1)}, bf16[2,64,16,128]{3,2,1,0:T(8,128)(2,1)}, u32[]{:S(2)}) copy-start(bf16[2,64,16,128]{3,2,1,0:T(8,128)(2,1)} %param.28) | copy-start | bytes 1572868
  7.2 109.8 %all-gather.12.cloned.1.call-start = ((), (), s32[]{:S(2)}) async-start(), calls=%async_computation.6 | async-start | bytes 4325376 | tf_op jit(solution)/shard_map/all_gather | solution.py:83
  17.2 59.8 %copy-start.3 = (bf16[2,64,2048]{2,1,0:T(8,128)(2,1)S(1)}, bf16[2,64,2048]{2,1,0:T(8,128)(2,1)}, u32[]{:S(2)}) copy-start(bf16[2,64,2048]{2,1,0:T(8,128)(2,1)} %param.20) | copy-start | bytes 1572868
  17.4 61.7 %copy-start.12 = (s32[64]{0:T(128)S(1)}, s32[64]{0:T(128)}, u32[]{:S(2)}) copy-start(s32[64]{0:T(128)} %param.31) | copy-start | bytes 772
  17.4 61.7 %copy-start.11 = (s32[32,64]{1,0:T(8,128)S(1)}, s32[32,64]{1,0:T(8,128)}, u32[]{:S(2)}) copy-start(s32[32,64]{1,0:T(8,128)} %param.33) | copy-start | bytes 24580
  17.4 61.8 %copy-start.13 = (s32[64]{0:T(128)S(1)}, s32[64]{0:T(128)}, u32[]{:S(2)}) copy-start(s32[64]{0:T(128)} %param.32) | copy-start | bytes 772
  18.3 54.5 %all-to-all-start = ((bf16[2,2,1,32,16,128]{5,4,1,0,2,3:T(8,128)(2,1)}), bf16[2,2,1,32,16,128]{5,4,1,0,2,3:T(8,128)(2,1)S(1)}, u32[]{:S(2)}, u32[]{:S(2)}) async-start(bf16[2,2,1,32,16,128]{5,4,1,0,2,3:T(8,128)(2,1)} %copy.123), calls=%async_computation | async-start | bytes 1048576 | tf_op jit(solution)/shard_map/all_to_all | solution.py:135
  72.8 42.7 %all-to-all-start.1 = ((bf16[2,2,1,32,16,128]{5,4,1,0,2,3:T(8,128)(2,1)}), bf16[2,2,1,32,16,128]{5,4,1,0,2,3:T(8,128)(2,1)S(1)}, u32[]{:S(2)}, u32[]{:S(2)}) async-start(bf16[2,2,1,32,16,128]{5,4,1,0,2,3:T(8,128)(2,1)} %copy.125), calls=%async_computation.1 | async-start | bytes 1048576 | tf_op jit(solution)/shard_map/all_to_all | solution.py:134
  127.7 55.9 %all-to-all-start.2 = ((bf16[16,2,128,128]{2,3,1,0:T(8,128)(2,1)}), bf16[16,2,128,128]{2,3,1,0:T(8,128)(2,1)S(1)}, u32[]{:S(2)}, u32[]{:S(2)}) async-start(bf16[16,2,128,128]{2,3,1,0:T(8,128)(2,1)} %bitcast.215), calls=%async_computation.2 | async-start | bytes 2097152 | tf_op jit(solution)/shard_map/all_to_all | solution.py:179
  134.4 160.4 %all-gather.10.cloned.1.call-start = ((), (), s32[]{:S(2)}) async-start(), calls=%async_computation.5 | async-start | bytes 8650752 | tf_op jit(solution)/shard_map/all_gather | solution.py:199
  134.4 27.6 %copy-start.9 = (f32[2,128]{1,0:T(2,128)S(1)}, f32[2,128]{1,0:T(2,128)}, u32[]{:S(2)}) copy-start(f32[2,128]{1,0:T(2,128)} %param.23) | copy-start | bytes 3076
  134.5 27.6 %copy-start.10 = (f32[2,128]{1,0:T(2,128)S(1)}, f32[2,128]{1,0:T(2,128)}, u32[]{:S(2)}) copy-start(f32[2,128]{1,0:T(2,128)} %param.24) | copy-start | bytes 3076
  134.5 27.9 %copy-start.5 = (bf16[2,2,1,32,16,128]{5,4,3,1,0,2:T(8,128)(2,1)S(1)}, bf16[2,2,1,32,16,128]{5,4,3,1,0,2:T(8,128)(2,1)}, u32[]{:S(2)}) copy-start(bf16[2,2,1,32,16,128]{5,4,3,1,0,2:T(8,128)(2,1)} %copy.126) | copy-start | bytes 1572868
  137.7 25.6 %copy-start.4 = (bf16[2,2,1,32,16,128]{5,4,3,1,0,2:T(8,128)(2,1)S(1)}, bf16[2,2,1,32,16,128]{5,4,3,1,0,2:T(8,128)(2,1)}, u32[]{:S(2)}) copy-start(bf16[2,2,1,32,16,128]{5,4,3,1,0,2:T(8,128)(2,1)} %copy.124) | copy-start | bytes 1572868
  163.7 40.6 %copy-start.6 = (f32[2,2048]{1,0:T(2,128)S(1)}, f32[2,2048]{1,0:T(2,128)}, u32[]{:S(2)}) copy-start(f32[2,2048]{1,0:T(2,128)} %param.25) | copy-start | bytes 49156
  183.6 21.1 %copy-start.7 = (f32[2,2048]{1,0:T(2,128)S(1)}, f32[2,2048]{1,0:T(2,128)}, u32[]{:S(2)}) copy-start(f32[2,2048]{1,0:T(2,128)} %param.26) | copy-start | bytes 49156
  185.6 22.5 %copy-start.8 = (s32[2048]{0:T(1024)S(1)}, s32[2048]{0:T(1024)}, u32[]{:S(2)}) copy-start(s32[2048]{0:T(1024)} %param.34) | copy-start | bytes 24580
  204.0 4.4 copy-start.2
  205.7 166.6 %all-gather.8.cloned.1.call-start = ((), (), s32[]{:S(2)}) async-start(), calls=%async_computation.4 | async-start | bytes 8650752 | tf_op jit(solution)/shard_map/all_gather | solution.py:199
  379.1 1.2 copy-start.1
  385.5 24.2 %all-to-all-start.3 = ((f32[32,1,1152]{2,1,0:T(1,128)}), f32[32,1,1152]{2,1,0:T(1,128)S(1)}, u32[]{:S(2)}, u32[]{:S(2)}) async-start(f32[32,1,1152]{2,1,0:T(1,128)} %reshape.599), calls=%async_computation.3 | async-start | bytes 294912 | tf_op jit(solution)/shard_map/all_to_all | solution.py:230
Sparse Core Ops, SparseCore 0:
  10.1 106.8 all-gather.11
  205.9 88.9 all-gather.9
  297.0 75.3 all-gather.7
